TPU v7x, 128 devices: a whole 4x4x4 slice. The times are simulated.
128 devices in a mesh: row: 16 (over x, y_hi, core), col: 8 (over z, y_lo).
Axes of the slice: x: 4, y: 4 (y_hi: 2, y_lo: 2; y = y_hi * 2 + y_lo), z: 4, core: 2. Of those that a mesh axis runs over, the one named last changes fastest.
Arguments:
- band_cells: float32 [3, 1024, 2], P(None, ('row', 'col')), may hold values from 0 to 1
- cell_counts: int32 [1024], P(('row', 'col')), may hold values from 1 to 2, as said below
- cell_assign: int32 [1024], P(('row', 'col')), may hold values from 0 to 1023, as said below
- wake_pos: float32 [3, 1048576], P(None, ('row', 'col')), may hold values from 0 to 1
- wake_strength: float32 [3, 1048576], P(None, ('row', 'col')), may hold values from -0.005859375 to 0.005859375
- wake_core: float32 [1, 1048576], P(None, ('row', 'col')), may hold values from 0.05 to 0.15
Outputs:
- velocity: float32 [3, 1024, 2], P(None, ('row', 'col'))
- gradient: float32 [9, 1024, 2], P(None, ('row', 'col'))
Inputs may be any that keep to these rules, and one draw needn't show every extreme that they name: `cell_counts`: each band cell holds its live particles in its first slots; some cell is full in every draw. `cell_assign`: A permutation of the cells. The cells of the device with index d along row+col go to positions q with q // 64 == d // 8; at most 1 of them land in the positions of any one device (q // 8); where 8 is a multiple of 8, exactly 1 land in the positions of each device of the group, else some pair of devices reaches 1.
All inputs are finite; a program needn't handle non-finite values.
Results may differ from a plain program's by a relative error of at most 0.0003.
Values sent between devices are 32-bit elements; how exact they have to be, the bound alone decides.
No kernel may reach another device: no remote copies, remote signals or barrier semaphores. Data moves between devices by JAX's collectives and lax.ppermute only.
A program may use at most 64 MiB of HBM per device.

v0:
```python
import math

import jax
import jax.numpy as jnp
from jax import lax
from jax.sharding import PartitionSpec as P

HIGHEST = lax.Precision.HIGHEST


def block_sums(target_pos, source_pos, source_str, source_core):
    delta_x = target_pos[0][:, None] - source_pos[0][None, :]
    delta_y = target_pos[1][:, None] - source_pos[1][None, :]
    delta_z = target_pos[2][:, None] - source_pos[2][None, :]
    radius_sq = (
        delta_x * delta_x
        + delta_y * delta_y
        + delta_z * delta_z
        + source_core[0][None, :] * source_core[0][None, :]
    )
    inverse = lax.rsqrt(radius_sq)
    kernel_three = inverse * inverse * inverse
    kernel_five = kernel_three * inverse * inverse
    alpha_x = source_str[0][None, :]
    alpha_y = source_str[1][None, :]
    alpha_z = source_str[2][None, :]
    cross_x = delta_y * alpha_z - delta_z * alpha_y
    cross_y = delta_z * alpha_x - delta_x * alpha_z
    cross_z = delta_x * alpha_y - delta_y * alpha_x
    terms_list = [
        kernel_three * cross_x,
        kernel_three * cross_y,
        kernel_three * cross_z,
        kernel_three * alpha_x,
        kernel_three * alpha_y,
        kernel_three * alpha_z,
    ]
    for along in (delta_x, delta_y, delta_z):
        for cross in (cross_x, cross_y, cross_z):
            terms_list.append(kernel_five * along * cross)
    return jnp.stack([jnp.sum(term, axis=1) for term in terms_list])


def pair_sums(target_pos, source_pos, source_str, source_core):
    source_total = source_pos.shape[1]
    block_width = math.gcd(source_total, max(512, 1048576 // target_pos.shape[1]))
    block_steps = source_total // block_width

    def one_block(running, block_index):
        offset = block_index * block_width
        part_pos = lax.dynamic_slice_in_dim(source_pos, offset, block_width, 1)
        part_str = lax.dynamic_slice_in_dim(source_str, offset, block_width, 1)
        part_core = lax.dynamic_slice_in_dim(source_core, offset, block_width, 1)
        return (running + block_sums(target_pos, part_pos, part_str, part_core), None)

    start_sums = jnp.zeros((15, target_pos.shape[1]), jnp.float32)
    running, unused = lax.scan(one_block, start_sums, jnp.arange(block_steps, dtype=jnp.int32))
    return running


def combine_rows(kernel_sums):
    biot_scale = -1.0 / (4.0 * math.pi)
    swirl_x, swirl_y, swirl_z = (kernel_sums[3], kernel_sums[4], kernel_sums[5])
    zero_row = jnp.zeros_like(swirl_x)
    levi_terms = [
        [zero_row, swirl_z, -swirl_y],
        [-swirl_z, zero_row, swirl_x],
        [swirl_y, -swirl_x, zero_row],
    ]
    out_rows = [
        biot_scale * kernel_sums[0],
        biot_scale * kernel_sums[1],
        biot_scale * kernel_sums[2],
    ]
    for comp_m in range(3):
        for comp_n in range(3):
            out_rows.append(
                biot_scale
                * (levi_terms[comp_m][comp_n] - 3.0 * kernel_sums[6 + comp_n * 3 + comp_m])
            )
    return jnp.stack(out_rows)


def apply_mask(finished_rows, slot_counts, slot_cap):
    slot_ids = jnp.arange(slot_cap).astype(slot_counts.dtype)
    alive_mask = (slot_ids[None, :] < slot_counts[:, None]).astype(jnp.float32).reshape(-1)
    masked = finished_rows * alive_mask[None, :]
    cell_total = slot_counts.shape[0]
    return (
        masked[0:3].reshape(3, cell_total, slot_cap),
        masked[3:12].reshape(9, cell_total, slot_cap),
    )


def per_device(band_cells, cell_counts, cell_assign, wake_pos, wake_strength, wake_core):
    col_devs = lax.axis_size("col")
    cell_total = band_cells.shape[1]
    slot_cap = band_cells.shape[2]
    block_cells = cell_total * col_devs
    counts_float = cell_counts.astype(jnp.float32)
    slot_width = max(1, cell_total // col_devs)
    local_order = cell_assign % block_cells
    target_dev = local_order // cell_total
    target_slot = local_order % cell_total
    cell_ids = jnp.arange(cell_total, dtype=jnp.int32)
    earlier_same = (target_dev[None, :] == target_dev[:, None]) & (
        cell_ids[None, :] < cell_ids[:, None]
    )
    slot_rank = jnp.sum(earlier_same.astype(jnp.int32), axis=1)
    send_index = target_dev * slot_width + slot_rank
    outgoing_map = (
        send_index[None, :] == jnp.arange(col_devs * slot_width, dtype=jnp.int32)[:, None]
    ).astype(jnp.float32)
    outgoing = jnp.einsum("st,ftc->fsc", outgoing_map, band_cells, precision=HIGHEST)
    routing = jnp.stack(
        [
            jnp.dot(outgoing_map, target_slot.astype(jnp.float32) + 1.0, precision=HIGHEST) - 1.0,
            jnp.dot(outgoing_map, counts_float, precision=HIGHEST),
        ]
    )
    incoming, routed = (
        lax.all_to_all(outgoing, "col", split_axis=1, concat_axis=1, tiled=True),
        lax.all_to_all(routing, "col", split_axis=1, concat_axis=1, tiled=True),
    )
    settle_map = (routed[0][None, :] == jnp.arange(cell_total, dtype=jnp.float32)[:, None]).astype(
        jnp.float32
    )
    own_cells = jnp.einsum("ts,fsc->ftc", settle_map, incoming, precision=HIGHEST)
    own_counts = jnp.dot(settle_map, routed[1], precision=HIGHEST)
    target_block, block_counts = (
        lax.all_gather(own_cells, "col", axis=1, tiled=True),
        lax.all_gather(own_counts, "col", axis=0, tiled=True),
    )
    target_pos = target_block.reshape(3, -1)
    local_sums = pair_sums(
        target_pos,
        lax.all_gather(wake_pos, "row", axis=1, tiled=True),
        lax.all_gather(wake_strength, "row", axis=1, tiled=True),
        lax.all_gather(wake_core, "row", axis=1, tiled=True),
    )
    own_rows = lax.psum_scatter(local_sums, "col", scatter_dimension=1, tiled=True)
    finished_rows = combine_rows(own_rows)
    return apply_mask(finished_rows, own_counts, slot_cap)


def solution(mesh):
    placed = (
        P(None, ("row", "col"), None),
        P(("row", "col")),
        P(("row", "col")),
        P(None, ("row", "col")),
        P(None, ("row", "col")),
        P(None, ("row", "col")),
    )
    return jax.shard_map(
        per_device,
        mesh=mesh,
        in_specs=placed,
        out_specs=(P(None, ("row", "col"), None), P(None, ("row", "col"), None)),
        check_vma=False,
    )
```

profile of v0, /device:TPU:1, one launch (start us, length us, event | category | flops | bytes accessed | tf_op | source)
XLA Modules:
  0.0 387.1 jit_solution(16849344204659096171)
XLA Ops:
  11.1 6.9 %all-to-all-start.1 = ((f32[2,8,1]{0,2,1:T(1,128)}), f32[2,8,1]{0,2,1:T(1,128)S(1)}, u32[]{:S(2)}, u32[]{:S(2)}) async-start(f32[2,8,1]{0,2,1:T(1,128)} %copy.46), calls=%async_computation.1 | async-start | bytes 8192 | tf_op jit(solution)/shard_map/all_to_all | solution.py:123
  18.2 26.8 %all_gather.14 = f32[1,131072]{1,0:T(1,128)S(1)} all-gather(f32[1,8192]{1,0:T(1,128)} %param.13), channel_id=1, replica_groups=mesh['row'=16,'col'=8] {'row'}, dimensions={1}, use_global_device_ids=true | all-gather | bytes 557056 | tf_op jit(solution)/shard_map/all_gather | solution.py:139
  45.6 4.7 %all-to-all-start = ((f32[3,8,2]{0,2,1:T(2,128)}), f32[3,8,2]{0,2,1:T(2,128)S(1)}, u32[]{:S(2)}, u32[]{:S(2)}) async-start(f32[3,8,2]{0,2,1:T(2,128)} %copy.45), calls=%async_computation | async-start | bytes 16384 | tf_op jit(solution)/shard_map/all_to_all | solution.py:122
  50.7 4.7 %all-to-all-done = f32[3,8,2]{0,2,1:T(2,128)S(1)} async-done(((f32[3,8,2]{0,2,1:T(2,128)}), f32[3,8,2]{0,2,1:T(2,128)S(1)}, u32[]{:S(2)}, u32[]{:S(2)}) %all-to-all-start) | async-done | bytes 224 | tf_op jit(solution)/shard_map/all_to_all | solution.py:122
  55.7 22.2 %all_gather.12 = f32[3,64,2]{0,2,1:T(2,128)S(1)} all-gather(f32[3,8,2]{0,2,1:T(2,128)S(1)} %copy.48), channel_id=1, replica_groups=mesh['row'=16,'col'=8] {'col'}, dimensions={1}, use_global_device_ids=true | all-gather | bytes 1728 | tf_op jit(solution)/shard_map/all_gather | solution.py:131
  77.9 35.2 %all-gather.5.cloned.1.call-done = f32[3,131072]{1,0:T(4,128)} async-done(((f32[3,8192]{1,0:T(4,128)}), f32[3,131072]{1,0:T(4,128)}) %all-gather.5.cloned.1.call-update) | async-done | bytes 1572880 | tf_op jit(solution)/shard_map/all_gather | solution.py:138
  113.1 233.6 %while.11 = (s32[]{:T(128)}, f32[15,128]{1,0:T(8,128)S(1)}, f32[3,128]{1,0:T(4,128)S(1)}, s32[16]{0:T(128)S(1)}, f32[3,131072]{1,0:T(4,128)}, /*index=5*/f32[1,1...) while((s32[]{:T(128)}, f32[15,128]{1,0:T(8,128)S(1)}, ...), condition=%wide.region_17.18_spmd.clone, body=%wide.region_1.17_spmd.clone.sunk | while | flops 57681800 | bytes 739065 | solution.py:57
  115.6 1.3 constant_dynamic-slice_fusion.3
  116.9 10.7 %fusion.80 = (f32[128]{0:T(128)S(1)}, f32[128]{0:T(128)S(1)}, f32[128]{0:T(128)S(1)}, f32[128]{0:T(128)S(1)}, f32[128]{0:T(128)S(1)}, /*index=5*/f32[128]{0:T(12...) fusion(f32[8192]{0:T(1024)S(1)} %bitcast.118, ...), kind=kLoop, calls=%fused_computation.28.clone.1 | loop fusion | flops 57669760 | bytes 238592 | tf_op jit(solution)/shard_map/while/body/eval_jaxpr/reduce_sum | solution.py:41
  131.5 10.7 %fusion.80 = (f32[128]{0:T(128)S(1)}, f32[128]{0:T(128)S(1)}, f32[128]{0:T(128)S(1)}, f32[128]{0:T(128)S(1)}, f32[128]{0:T(128)S(1)}, /*index=5*/f32[128]{0:T(12...) fusion(f32[8192]{0:T(1024)S(1)} %bitcast.118, ...), kind=kLoop, calls=%fused_computation.28.clone.1 | loop fusion | flops 57669760 | bytes 238592 | tf_op jit(solution)/shard_map/while/body/eval_jaxpr/reduce_sum | solution.py:41
  146.1 10.7 %fusion.80 = (f32[128]{0:T(128)S(1)}, f32[128]{0:T(128)S(1)}, f32[128]{0:T(128)S(1)}, f32[128]{0:T(128)S(1)}, f32[128]{0:T(128)S(1)}, /*index=5*/f32[128]{0:T(12...) fusion(f32[8192]{0:T(1024)S(1)} %bitcast.118, ...), kind=kLoop, calls=%fused_computation.28.clone.1 | loop fusion | flops 57669760 | bytes 238592 | tf_op jit(solution)/shard_map/while/body/eval_jaxpr/reduce_sum | solution.py:41
  159.4 1.3 constant_dynamic-slice_fusion.3
  160.7 10.7 %fusion.80 = (f32[128]{0:T(128)S(1)}, f32[128]{0:T(128)S(1)}, f32[128]{0:T(128)S(1)}, f32[128]{0:T(128)S(1)}, f32[128]{0:T(128)S(1)}, /*index=5*/f32[128]{0:T(12...) fusion(f32[8192]{0:T(1024)S(1)} %bitcast.118, ...), kind=kLoop, calls=%fused_computation.28.clone.1 | loop fusion | flops 57669760 | bytes 238592 | tf_op jit(solution)/shard_map/while/body/eval_jaxpr/reduce_sum | solution.py:41
  175.3 10.7 %fusion.80 = (f32[128]{0:T(128)S(1)}, f32[128]{0:T(128)S(1)}, f32[128]{0:T(128)S(1)}, f32[128]{0:T(128)S(1)}, f32[128]{0:T(128)S(1)}, /*index=5*/f32[128]{0:T(12...) fusion(f32[8192]{0:T(1024)S(1)} %bitcast.118, ...), kind=kLoop, calls=%fused_computation.28.clone.1 | loop fusion | flops 57669760 | bytes 238592 | tf_op jit(solution)/shard_map/while/body/eval_jaxpr/reduce_sum | solution.py:41
  188.6 1.3 constant_dynamic-slice_fusion.3
  189.9 10.7 %fusion.80 = (f32[128]{0:T(128)S(1)}, f32[128]{0:T(128)S(1)}, f32[128]{0:T(128)S(1)}, f32[128]{0:T(128)S(1)}, f32[128]{0:T(128)S(1)}, /*index=5*/f32[128]{0:T(12...) fusion(f32[8192]{0:T(1024)S(1)} %bitcast.118, ...), kind=kLoop, calls=%fused_computation.28.clone.1 | loop fusion | flops 57669760 | bytes 238592 | tf_op jit(solution)/shard_map/while/body/eval_jaxpr/reduce_sum | solution.py:41
  202.0 1.3 fusion.79
  204.5 10.7 %fusion.80 = (f32[128]{0:T(128)S(1)}, f32[128]{0:T(128)S(1)}, f32[128]{0:T(128)S(1)}, f32[128]{0:T(128)S(1)}, f32[128]{0:T(128)S(1)}, /*index=5*/f32[128]{0:T(12...) fusion(f32[8192]{0:T(1024)S(1)} %bitcast.118, ...), kind=kLoop, calls=%fused_computation.28.clone.1 | loop fusion | flops 57669760 | bytes 238592 | tf_op jit(solution)/shard_map/while/body/eval_jaxpr/reduce_sum | solution.py:41
  217.8 1.3 constant_dynamic-slice_fusion.3
  219.1 10.7 %fusion.80 = (f32[128]{0:T(128)S(1)}, f32[128]{0:T(128)S(1)}, f32[128]{0:T(128)S(1)}, f32[128]{0:T(128)S(1)}, f32[128]{0:T(128)S(1)}, /*index=5*/f32[128]{0:T(12...) fusion(f32[8192]{0:T(1024)S(1)} %bitcast.118, ...), kind=kLoop, calls=%fused_computation.28.clone.1 | loop fusion | flops 57669760 | bytes 238592 | tf_op jit(solution)/shard_map/while/body/eval_jaxpr/reduce_sum | solution.py:41
  233.7 10.7 %fusion.80 = (f32[128]{0:T(128)S(1)}, f32[128]{0:T(128)S(1)}, f32[128]{0:T(128)S(1)}, f32[128]{0:T(128)S(1)}, f32[128]{0:T(128)S(1)}, /*index=5*/f32[128]{0:T(12...) fusion(f32[8192]{0:T(1024)S(1)} %bitcast.118, ...), kind=kLoop, calls=%fused_computation.28.clone.1 | loop fusion | flops 57669760 | bytes 238592 | tf_op jit(solution)/shard_map/while/body/eval_jaxpr/reduce_sum | solution.py:41
  247.1 1.3 constant_dynamic-slice_fusion.3
  248.3 10.7 %fusion.80 = (f32[128]{0:T(128)S(1)}, f32[128]{0:T(128)S(1)}, f32[128]{0:T(128)S(1)}, f32[128]{0:T(128)S(1)}, f32[128]{0:T(128)S(1)}, /*index=5*/f32[128]{0:T(12...) fusion(f32[8192]{0:T(1024)S(1)} %bitcast.118, ...), kind=kLoop, calls=%fused_computation.28.clone.1 | loop fusion | flops 57669760 | bytes 238592 | tf_op jit(solution)/shard_map/while/body/eval_jaxpr/reduce_sum | solution.py:41
  262.9 10.7 %fusion.80 = (f32[128]{0:T(128)S(1)}, f32[128]{0:T(128)S(1)}, f32[128]{0:T(128)S(1)}, f32[128]{0:T(128)S(1)}, f32[128]{0:T(128)S(1)}, /*index=5*/f32[128]{0:T(12...) fusion(f32[8192]{0:T(1024)S(1)} %bitcast.118, ...), kind=kLoop, calls=%fused_computation.28.clone.1 | loop fusion | flops 57669760 | bytes 238592 | tf_op jit(solution)/shard_map/while/body/eval_jaxpr/reduce_sum | solution.py:41
  277.5 10.7 %fusion.80 = (f32[128]{0:T(128)S(1)}, f32[128]{0:T(128)S(1)}, f32[128]{0:T(128)S(1)}, f32[128]{0:T(128)S(1)}, f32[128]{0:T(128)S(1)}, /*index=5*/f32[128]{0:T(12...) fusion(f32[8192]{0:T(1024)S(1)} %bitcast.118, ...), kind=kLoop, calls=%fused_computation.28.clone.1 | loop fusion | flops 57669760 | bytes 238592 | tf_op jit(solution)/shard_map/while/body/eval_jaxpr/reduce_sum | solution.py:41
  292.1 10.7 %fusion.80 = (f32[128]{0:T(128)S(1)}, f32[128]{0:T(128)S(1)}, f32[128]{0:T(128)S(1)}, f32[128]{0:T(128)S(1)}, f32[128]{0:T(128)S(1)}, /*index=5*/f32[128]{0:T(12...) fusion(f32[8192]{0:T(1024)S(1)} %bitcast.118, ...), kind=kLoop, calls=%fused_computation.28.clone.1 | loop fusion | flops 57669760 | bytes 238592 | tf_op jit(solution)/shard_map/while/body/eval_jaxpr/reduce_sum | solution.py:41
  306.7 10.7 %fusion.80 = (f32[128]{0:T(128)S(1)}, f32[128]{0:T(128)S(1)}, f32[128]{0:T(128)S(1)}, f32[128]{0:T(128)S(1)}, f32[128]{0:T(128)S(1)}, /*index=5*/f32[128]{0:T(12...) fusion(f32[8192]{0:T(1024)S(1)} %bitcast.118, ...), kind=kLoop, calls=%fused_computation.28.clone.1 | loop fusion | flops 57669760 | bytes 238592 | tf_op jit(solution)/shard_map/while/body/eval_jaxpr/reduce_sum | solution.py:41
  321.3 10.7 %fusion.80 = (f32[128]{0:T(128)S(1)}, f32[128]{0:T(128)S(1)}, f32[128]{0:T(128)S(1)}, f32[128]{0:T(128)S(1)}, f32[128]{0:T(128)S(1)}, /*index=5*/f32[128]{0:T(12...) fusion(f32[8192]{0:T(1024)S(1)} %bitcast.118, ...), kind=kLoop, calls=%fused_computation.28.clone.1 | loop fusion | flops 57669760 | bytes 238592 | tf_op jit(solution)/shard_map/while/body/eval_jaxpr/reduce_sum | solution.py:41
  334.7 1.3 constant_dynamic-slice_fusion.3
  335.9 10.7 %fusion.80 = (f32[128]{0:T(128)S(1)}, f32[128]{0:T(128)S(1)}, f32[128]{0:T(128)S(1)}, f32[128]{0:T(128)S(1)}, f32[128]{0:T(128)S(1)}, /*index=5*/f32[128]{0:T(12...) fusion(f32[8192]{0:T(1024)S(1)} %bitcast.118, ...), kind=kLoop, calls=%fused_computation.28.clone.1 | loop fusion | flops 57669760 | bytes 238592 | tf_op jit(solution)/shard_map/while/body/eval_jaxpr/reduce_sum | solution.py:41
  347.6 30.1 %reduce-scatter.4.cloned.1.call-done = f32[16,15]{1,0:T(8,128)} async-done(((f32[128,15]{1,0:T(8,128)}), f32[16,15]{1,0:T(8,128)}) %reduce-scatter.4.cloned.1.call-update) | async-done | bytes 976
  377.7 1.3 fusion.34
  (123 shorter events, 50.0 us)
Async XLA Ops:
  7.2 10.9 %copy-start = (f32[3,8,2]{1,2,0:T(2,128)S(1)}, f32[3,8,2]{1,2,0:T(2,128)}, u32[]{:S(2)}) copy-start(f32[3,8,2]{1,2,0:T(2,128)} %param.8) | copy-start | bytes 580
  7.2 70.7 %all-gather.3.cloned.1.call-start = ((), (), s32[]{:S(2)}) async-start(), calls=%async_computation.3 | async-start | bytes 2228224 | tf_op jit(solution)/shard_map/all_gather | solution.py:137
  7.9 105.2 %all-gather.5.cloned.1.call-start = ((), (), s32[]{:S(2)}) async-start(), calls=%async_computation.4 | async-start | bytes 2228224 | tf_op jit(solution)/shard_map/all_gather | solution.py:138
  11.1 34.5 %all-to-all-start.1 = ((f32[2,8,1]{0,2,1:T(1,128)}), f32[2,8,1]{0,2,1:T(1,128)S(1)}, u32[]{:S(2)}, u32[]{:S(2)}) async-start(f32[2,8,1]{0,2,1:T(1,128)} %copy.46), calls=%async_computation.1 | async-start | bytes 8192 | tf_op jit(solution)/shard_map/all_to_all | solution.py:123
  45.6 9.8 %all-to-all-start = ((f32[3,8,2]{0,2,1:T(2,128)}), f32[3,8,2]{0,2,1:T(2,128)S(1)}, u32[]{:S(2)}, u32[]{:S(2)}) async-start(f32[3,8,2]{0,2,1:T(2,128)} %copy.45), calls=%async_computation | async-start | bytes 16384 | tf_op jit(solution)/shard_map/all_to_all | solution.py:122
  50.3 327.4 %reduce-scatter.4.cloned.1.call-start = ((), (), s32[]{:S(2)}) async-start(), calls=%async_computation.5 | async-start | bytes 73728
Sparse Core Ops, SparseCore 0:
  10.4 52.9 all-gather.2
  65.8 47.2 all-gather.4
  347.6 30.0 reduce-scatter.3
where the time goes:
time: 393 us; the launch traced here: 387 us
  other arithmetic  194 us (49%)
  waiting for transfers between devices  71.4 us (18%)
  blocking collectives  48.9 us (12%)
  local copies, waits for them, and re-layouts  34.6 us (9%)
  between operations  13.8 us (4%)
  starting transfers between devices  11.7 us (3%)
  loops' own time  11 us (3%)
    reduce_sum x16, other arithmetic, block_sums(): return jnp.stack([jnp.sum(term, axis=1) for term in terms_list])  172 us
    all_gather x1, waiting for transfers between devices, per_device(): lax.all_gather(wake_strength, 'row', axis=1, tiled=True)  35.2 us
    unnamed x4, waiting for transfers between devices  31.5 us
    all_gather x1, blocking collectives, per_device(): lax.all_gather(wake_core, 'row', axis=1, tiled=True)  26.8 us
    all_gather x1, blocking collectives, per_device(): lax.all_gather(own_cells, 'col', axis=1, tiled=True)  22.2 us
    slice x16, other arithmetic, block_sums(): delta_x = target_pos[0][:, None] - source_pos[0][None, :]  20.3 us
    slice x16, local copies, waits for them, and re-layouts, block_sums(): alpha_z = source_str[2][None, :]  20.3 us
    another operation x1, loops' own time, pair_sums(): lax.scan(one_block, start_sums, jnp.arange(block_steps, dtype=jnp.int32))  11 us
  transfers between devices with their start and end apart: 5, of which 3 were waited for; matrix products, arithmetic and copies ran while one was open for 1% of the time, Pallas kernels for 0%

commit v1 on v0

--- a/solution.py
+++ b/solution.py
@@ -93,52 +93,35 @@
 
 
 def per_device(band_cells, cell_counts, cell_assign, wake_pos, wake_strength, wake_core):
+    axes = ("row", "col")
     col_devs = lax.axis_size("col")
     cell_total = band_cells.shape[1]
     slot_cap = band_cells.shape[2]
-    block_cells = cell_total * col_devs
-    counts_float = cell_counts.astype(jnp.float32)
-    slot_width = max(1, cell_total // col_devs)
-    local_order = cell_assign % block_cells
-    target_dev = local_order // cell_total
-    target_slot = local_order % cell_total
-    cell_ids = jnp.arange(cell_total, dtype=jnp.int32)
-    earlier_same = (target_dev[None, :] == target_dev[:, None]) & (
-        cell_ids[None, :] < cell_ids[:, None]
+    group_cells = cell_total * col_devs
+    packed = jnp.concatenate(
+        [
+            band_cells.transpose(1, 0, 2).reshape(cell_total, 3 * slot_cap),
+            cell_counts.astype(jnp.float32)[:, None],
+            cell_assign.astype(jnp.float32)[:, None],
+        ],
+        axis=1,
     )
-    slot_rank = jnp.sum(earlier_same.astype(jnp.int32), axis=1)
-    send_index = target_dev * slot_width + slot_rank
-    outgoing_map = (
-        send_index[None, :] == jnp.arange(col_devs * slot_width, dtype=jnp.int32)[:, None]
-    ).astype(jnp.float32)
-    outgoing = jnp.einsum("st,ftc->fsc", outgoing_map, band_cells, precision=HIGHEST)
-    routing = jnp.stack(
-        [
-            jnp.dot(outgoing_map, target_slot.astype(jnp.float32) + 1.0, precision=HIGHEST) - 1.0,
-            jnp.dot(outgoing_map, counts_float, precision=HIGHEST),
-        ]
-    )
-    incoming, routed = (
-        lax.all_to_all(outgoing, "col", split_axis=1, concat_axis=1, tiled=True),
-        lax.all_to_all(routing, "col", split_axis=1, concat_axis=1, tiled=True),
-    )
-    settle_map = (routed[0][None, :] == jnp.arange(cell_total, dtype=jnp.float32)[:, None]).astype(
-        jnp.float32
-    )
-    own_cells = jnp.einsum("ts,fsc->ftc", settle_map, incoming, precision=HIGHEST)
-    own_counts = jnp.dot(settle_map, routed[1], precision=HIGHEST)
-    target_block, block_counts = (
-        lax.all_gather(own_cells, "col", axis=1, tiled=True),
-        lax.all_gather(own_counts, "col", axis=0, tiled=True),
-    )
-    target_pos = target_block.reshape(3, -1)
-    local_sums = pair_sums(
-        target_pos,
-        lax.all_gather(wake_pos, "row", axis=1, tiled=True),
-        lax.all_gather(wake_strength, "row", axis=1, tiled=True),
-        lax.all_gather(wake_core, "row", axis=1, tiled=True),
-    )
-    own_rows = lax.psum_scatter(local_sums, "col", scatter_dimension=1, tiled=True)
+    every_cell = lax.all_gather(packed, axes, axis=0, tiled=True)
+    all_cells = every_cell.shape[0]
+    groups = all_cells // group_cells
+    grouped = every_cell.reshape(groups, group_cells, 3 * slot_cap + 2)
+    within = grouped[:, :, -1].astype(jnp.int32) % group_cells
+    position = jnp.arange(group_cells, dtype=jnp.int32)
+    chosen = within[:, None, :] == position[None, :, None]
+    relaid = jnp.sum(
+        jnp.where(chosen[:, :, :, None], grouped[:, None, :, : 3 * slot_cap + 1], 0.0), axis=2
+    ).reshape(all_cells, 3 * slot_cap + 1)
+    target_pos = relaid[:, : 3 * slot_cap].reshape(all_cells, 3, slot_cap)
+    target_pos = target_pos.transpose(1, 0, 2).reshape(3, all_cells * slot_cap)
+    device = lax.axis_index("row") * col_devs + lax.axis_index("col")
+    own_counts = lax.dynamic_slice_in_dim(relaid[:, 3 * slot_cap], device * cell_total, cell_total)
+    local_sums = pair_sums(target_pos, wake_pos, wake_strength, wake_core)
+    own_rows = lax.psum_scatter(local_sums, axes, scatter_dimension=1, tiled=True)
     finished_rows = combine_rows(own_rows)
     return apply_mask(finished_rows, own_counts, slot_cap)
 

time: 393 us -> 1220 us (3.10)
  waiting for transfers between devices: 71.4 us -> 633 us
  blocking collectives: 48.9 us -> 306 us
    unnamed x4 -> x2, waiting for transfers between devices: 31.5 us -> 633 us
    all_gather x2 -> x1, blocking collectives: 48.9 us -> 306 us  [per_device(): every_cell = lax.all_gather(packed, axes, axis=0, tiled=True)]
    all_gather x2 -> x0, waiting for transfers between devices: 35.2 us -> none  [the longest x1 35.2 us: per_device(): lax.all_gather(wake_strength, 'row', axis=1, tiled=True)]
    reduce_sum x16, other arithmetic: 172 us -> 187 us  [block_sums(): return jnp.stack([jnp.sum(term, axis=1) for term in terms_list])]
  transfers between devices with their start and end apart: 5 -> 1, of which waited for: 3 -> 1; matrix products, arithmetic and copies ran while one was open for 1% -> 0% of each run, Pallas kernels for 0% -> 0%
where the time goes in v1:
time: 1220 us; the launch traced here: 1200 us
  waiting for transfers between devices  633 us (52%)
  blocking collectives  306 us (25%)
  other arithmetic  206 us (17%)
  local copies, waits for them, and re-layouts  33 us (3%)
  between operations  14.1 us (1%)
    unnamed x2, waiting for transfers between devices  633 us
    all_gather x1, blocking collectives, per_device(): every_cell = lax.all_gather(packed, axes, axis=0, tiled=True)  306 us
    reduce_sum x16, other arithmetic, block_sums(): return jnp.stack([jnp.sum(term, axis=1) for term in terms_list])  187 us
  transfers between devices with their start and end apart: 1, of which 1 were waited for; matrix products, arithmetic and copies ran while one was open for 0% of the time, Pallas kernels for 0%

profile of v1, /device:TPU:1, one launch (start us, length us, event | category | flops | bytes accessed | tf_op | source)
XLA Modules:
  0.0 1202.6 jit_solution(9751047633105874884)
XLA Ops:
  8.7 305.7 %all_gather.3 = f32[1024,8]{1,0:T(8,128)S(1)} all-gather(f32[8,8]{1,0:T(8,128)S(1)} %copy.62), channel_id=1, replica_groups=mesh['row'=16,'col'=8] {'row','col'}, dimensions={0}, use_global_device_ids=true | all-gather | bytes 33024 | tf_op jit(solution)/shard_map/all_gather | solution.py:109
  315.1 1.0 select_reduce_fusion
  317.7 240.7 %while.11 = (s32[]{:T(128)}, f32[15,2048]{1,0:T(8,128)S(1)}, f32[3,2048]{1,0:T(4,128)S(1)}, s32[16]{0:T(128)S(1)}, f32[3,8192]{1,0:T(4,128)}, /*index=5*/f32[1,8...) while((s32[]{:T(128)}, f32[15,2048]{1,0:T(8,128)S(1)}, ...), condition=%wide.region_17.18_spmd.clone, body=%wide.region_1.17_spmd.clone.sunk | while | flops 57702920 | bytes 854257 | solution.py:57
  318.9 0.9 constant_dynamic-slice_fusion.3
  320.8 11.7 fusion.57
  334.0 0.9 constant_dynamic-slice_fusion.3
  335.8 11.7 fusion.57
  349.0 0.9 constant_dynamic-slice_fusion.3
  350.8 11.7 fusion.57
  364.1 0.9 constant_dynamic-slice_fusion.3
  365.9 11.7 fusion.57
  379.1 0.9 constant_dynamic-slice_fusion.3
  380.9 11.7 fusion.57
  394.2 0.9 constant_dynamic-slice_fusion.3
  396.0 11.7 fusion.57
  409.2 0.9 constant_dynamic-slice_fusion.3
  411.0 11.7 fusion.57
  424.2 0.9 constant_dynamic-slice_fusion.3
  426.1 11.7 fusion.57
  439.3 0.9 constant_dynamic-slice_fusion.3
  441.1 11.7 fusion.57
  456.1 11.7 fusion.57
  471.2 11.7 fusion.57
  486.2 11.7 fusion.57
  501.3 11.7 fusion.57
  516.3 11.7 fusion.57
  531.3 11.7 fusion.57
  544.6 0.9 constant_dynamic-slice_fusion.3
  546.4 11.7 fusion.57
  558.4 1.4 copy.84
  560.0 632.5 %reduce-scatter.4.cloned.1.call-done = f32[16,15]{1,0:T(8,128)} async-done(((f32[2048,15]{1,0:T(8,128)}), f32[16,15]{1,0:T(8,128)}) %reduce-scatter.4.cloned.1.call-update) | async-done | bytes 976
  1192.5 1.7 fusion.33
  (113 shorter events, 38.6 us)
Async XLA Ops:
  7.2 1185.4 %reduce-scatter.4.cloned.1.call-start = ((), (), s32[]{:S(2)}) async-start(), calls=%async_computation.1 | async-start | bytes 1056768
Sparse Core Ops, SparseCore 0:
  559.9 632.5 reduce-scatter.3

commit v2 on v1

--- a/solution.py
+++ b/solution.py
@@ -106,8 +106,11 @@
         ],
         axis=1,
     )
-    every_cell = lax.all_gather(packed, axes, axis=0, tiled=True)
-    all_cells = every_cell.shape[0]
+    devices = lax.axis_size("row") * col_devs
+    copies = jnp.broadcast_to(packed[None], (devices,) + packed.shape)
+    every_cell = lax.all_to_all(copies, axes, 0, 0, tiled=True)
+    all_cells = devices * cell_total
+    every_cell = every_cell.reshape(all_cells, packed.shape[1])
     groups = all_cells // group_cells
     grouped = every_cell.reshape(groups, group_cells, 3 * slot_cap + 2)
     within = grouped[:, :, -1].astype(jnp.int32) % group_cells
@@ -121,7 +124,9 @@
     device = lax.axis_index("row") * col_devs + lax.axis_index("col")
     own_counts = lax.dynamic_slice_in_dim(relaid[:, 3 * slot_cap], device * cell_total, cell_total)
     local_sums = pair_sums(target_pos, wake_pos, wake_strength, wake_core)
-    own_rows = lax.psum_scatter(local_sums, axes, scatter_dimension=1, tiled=True)
+    rows = local_sums.shape[0]
+    by_device = local_sums.reshape(rows, devices, cell_total * slot_cap).transpose(1, 0, 2)
+    own_rows = jnp.sum(lax.all_to_all(by_device, axes, 0, 0, tiled=True), axis=0)
     finished_rows = combine_rows(own_rows)
     return apply_mask(finished_rows, own_counts, slot_cap)
 

time: 1220 us -> 293 us (0.24); the launches traced: 1200 us -> 291 us
  waiting for transfers between devices: 633 us -> 23.3 us
  blocking collectives: 306 us -> 0 us
  starting transfers between devices: 0.04 us -> 16.2 us
  between operations: 14.1 us -> 0.81 us
    unnamed x2 -> x0, waiting for transfers between devices: 633 us -> none
    all_gather x1 -> x0, blocking collectives: 306 us -> none  [per_device(): every_cell = lax.all_gather(packed, axes, axis=0, tiled=True)]
    all_to_all x0 -> x2, waiting for transfers between devices: none -> 23.3 us  [the longest x1 13.5 us: per_device(): every_cell = lax.all_to_all(copies, axes, 0, 0, tiled=True)]
    all_to_all x0 -> x2, starting transfers between devices: none -> 16.2 us  [the longest x1 11.5 us: per_device(): every_cell = lax.all_to_all(copies, axes, 0, 0, tiled=True)]
  transfers between devices with their start and end apart: 1 -> 2, of which waited for: 1 -> 2; matrix products, arithmetic and copies ran while one was open for 0% -> 0% of each run, Pallas kernels for 0% -> 0%
where the time goes in v2:
time: 293 us; the launch traced here: 291 us
  other arithmetic  205 us (70%)
  local copies, waits for them, and re-layouts  35 us (12%)
  waiting for transfers between devices  23.3 us (8%)
  starting transfers between devices  16.2 us (6%)
  loops' own time  11.1 us (4%)
    reduce_sum x16, other arithmetic, block_sums(): return jnp.stack([jnp.sum(term, axis=1) for term in terms_list])  187 us
    slice x16, local copies, waits for them, and re-layouts, block_sums(): alpha_z = source_str[2][None, :]  14.3 us
    slice x16, other arithmetic, block_sums(): delta_x = target_pos[0][:, None] - source_pos[0][None, :]  14.2 us
    all_to_all x1, waiting for transfers between devices, per_device(): every_cell = lax.all_to_all(copies, axes, 0, 0, tiled=True)  13.5 us
    all_to_all x1, starting transfers between devices, per_device(): every_cell = lax.all_to_all(copies, axes, 0, 0, tiled=True)  11.5 us
    another operation x1, loops' own time, pair_sums(): lax.scan(one_block, start_sums, jnp.arange(block_steps, dtype=jnp.int32))  11.1 us
    all_to_all x1, waiting for transfers between devices, per_device(): lax.all_to_all(by_device, axes, 0, 0, tiled=True)  9.77 us
    dynamic_slice x16, local copies, waits for them, and re-layouts, pair_sums(): lax.scan(one_block, start_sums, jnp.arange(block_steps, dtype=jnp.int32))  9.38 us
  transfers between devices with their start and end apart: 2, of which 2 were waited for; matrix products, arithmetic and copies ran while one was open for 0% of the time, Pallas kernels for 0%

profile of v2, /device:TPU:1, one launch (start us, length us, event | category | flops | bytes accessed | tf_op | source)
XLA Modules:
  0.0 291.4 jit_solution(7636705153553218158)
XLA Ops:
  2.8 11.5 %all-to-all-start = ((f32[128,8,8]{1,2,0:T(8,128)}), f32[128,8,8]{1,2,0:T(8,128)S(1)}, u32[]{:S(2)}, u32[]{:S(2)}) async-start(f32[128,8,8]{1,2,0:T(8,128)} %broadcast_in_dim.44), calls=%async_computation | async-start | bytes 1048576 | tf_op jit(solution)/shard_map/all_to_all | solution.py:111
  14.4 13.5 %all-to-all-done = f32[128,8,8]{1,2,0:T(8,128)S(1)} async-done(((f32[128,8,8]{1,2,0:T(8,128)}), f32[128,8,8]{1,2,0:T(8,128)S(1)}, u32[]{:S(2)}, u32[]{:S(2)}) %all-to-all-start) | async-done | bytes 32800 | tf_op jit(solution)/shard_map/all_to_all | solution.py:111
  28.4 1.0 select_reduce_fusion
  30.9 240.4 %while.11 = (s32[]{:T(128)}, f32[15,2048]{1,0:T(8,128)S(1)}, f32[3,2048]{1,0:T(4,128)S(1)}, s32[16]{0:T(128)S(1)}, f32[3,8192]{1,0:T(4,128)}, /*index=5*/f32[1,8...) while((s32[]{:T(128)}, f32[15,2048]{1,0:T(8,128)S(1)}, ...), condition=%wide.region_17.18_spmd.clone, body=%wide.region_1.17_spmd.clone.sunk | while | flops 57702920 | bytes 854265 | solution.py:57
  32.2 0.9 fusion.56
  34.0 11.7 %fusion.58 = (f32[2048]{0:T(1024)S(1)}, f32[2048]{0:T(1024)S(1)}, f32[2048]{0:T(1024)S(1)}, f32[2048]{0:T(1024)S(1)}, f32[2048]{0:T(1024)S(1)}, /*index=5*/f32[2...) fusion(f32[512]{0:T(512)S(1)} %bitcast.126, ...), kind=kLoop, calls=%fused_computation.28.clone.1 | loop fusion | flops 57640960 | bytes 161792 | tf_op jit(solution)/shard_map/while/body/eval_jaxpr/reduce_sum | solution.py:41
  47.2 0.9 fusion.56
  49.0 11.7 %fusion.58 = (f32[2048]{0:T(1024)S(1)}, f32[2048]{0:T(1024)S(1)}, f32[2048]{0:T(1024)S(1)}, f32[2048]{0:T(1024)S(1)}, f32[2048]{0:T(1024)S(1)}, /*index=5*/f32[2...) fusion(f32[512]{0:T(512)S(1)} %bitcast.126, ...), kind=kLoop, calls=%fused_computation.28.clone.1 | loop fusion | flops 57640960 | bytes 161792 | tf_op jit(solution)/shard_map/while/body/eval_jaxpr/reduce_sum | solution.py:41
  64.0 11.7 %fusion.58 = (f32[2048]{0:T(1024)S(1)}, f32[2048]{0:T(1024)S(1)}, f32[2048]{0:T(1024)S(1)}, f32[2048]{0:T(1024)S(1)}, f32[2048]{0:T(1024)S(1)}, /*index=5*/f32[2...) fusion(f32[512]{0:T(512)S(1)} %bitcast.126, ...), kind=kLoop, calls=%fused_computation.28.clone.1 | loop fusion | flops 57640960 | bytes 161792 | tf_op jit(solution)/shard_map/while/body/eval_jaxpr/reduce_sum | solution.py:41
  79.1 11.7 %fusion.58 = (f32[2048]{0:T(1024)S(1)}, f32[2048]{0:T(1024)S(1)}, f32[2048]{0:T(1024)S(1)}, f32[2048]{0:T(1024)S(1)}, f32[2048]{0:T(1024)S(1)}, /*index=5*/f32[2...) fusion(f32[512]{0:T(512)S(1)} %bitcast.126, ...), kind=kLoop, calls=%fused_computation.28.clone.1 | loop fusion | flops 57640960 | bytes 161792 | tf_op jit(solution)/shard_map/while/body/eval_jaxpr/reduce_sum | solution.py:41
  94.1 11.7 %fusion.58 = (f32[2048]{0:T(1024)S(1)}, f32[2048]{0:T(1024)S(1)}, f32[2048]{0:T(1024)S(1)}, f32[2048]{0:T(1024)S(1)}, f32[2048]{0:T(1024)S(1)}, /*index=5*/f32[2...) fusion(f32[512]{0:T(512)S(1)} %bitcast.126, ...), kind=kLoop, calls=%fused_computation.28.clone.1 | loop fusion | flops 57640960 | bytes 161792 | tf_op jit(solution)/shard_map/while/body/eval_jaxpr/reduce_sum | solution.py:41
  109.1 11.7 %fusion.58 = (f32[2048]{0:T(1024)S(1)}, f32[2048]{0:T(1024)S(1)}, f32[2048]{0:T(1024)S(1)}, f32[2048]{0:T(1024)S(1)}, f32[2048]{0:T(1024)S(1)}, /*index=5*/f32[2...) fusion(f32[512]{0:T(512)S(1)} %bitcast.126, ...), kind=kLoop, calls=%fused_computation.28.clone.1 | loop fusion | flops 57640960 | bytes 161792 | tf_op jit(solution)/shard_map/while/body/eval_jaxpr/reduce_sum | solution.py:41
  122.3 0.9 fusion.56
  124.1 11.7 %fusion.58 = (f32[2048]{0:T(1024)S(1)}, f32[2048]{0:T(1024)S(1)}, f32[2048]{0:T(1024)S(1)}, f32[2048]{0:T(1024)S(1)}, f32[2048]{0:T(1024)S(1)}, /*index=5*/f32[2...) fusion(f32[512]{0:T(512)S(1)} %bitcast.126, ...), kind=kLoop, calls=%fused_computation.28.clone.1 | loop fusion | flops 57640960 | bytes 161792 | tf_op jit(solution)/shard_map/while/body/eval_jaxpr/reduce_sum | solution.py:41
  137.3 0.9 fusion.56
  139.2 11.7 %fusion.58 = (f32[2048]{0:T(1024)S(1)}, f32[2048]{0:T(1024)S(1)}, f32[2048]{0:T(1024)S(1)}, f32[2048]{0:T(1024)S(1)}, f32[2048]{0:T(1024)S(1)}, /*index=5*/f32[2...) fusion(f32[512]{0:T(512)S(1)} %bitcast.126, ...), kind=kLoop, calls=%fused_computation.28.clone.1 | loop fusion | flops 57640960 | bytes 161792 | tf_op jit(solution)/shard_map/while/body/eval_jaxpr/reduce_sum | solution.py:41
  152.4 0.9 fusion.56
  154.2 11.7 %fusion.58 = (f32[2048]{0:T(1024)S(1)}, f32[2048]{0:T(1024)S(1)}, f32[2048]{0:T(1024)S(1)}, f32[2048]{0:T(1024)S(1)}, f32[2048]{0:T(1024)S(1)}, /*index=5*/f32[2...) fusion(f32[512]{0:T(512)S(1)} %bitcast.126, ...), kind=kLoop, calls=%fused_computation.28.clone.1 | loop fusion | flops 57640960 | bytes 161792 | tf_op jit(solution)/shard_map/while/body/eval_jaxpr/reduce_sum | solution.py:41
  167.4 0.9 fusion.56
  169.2 11.7 %fusion.58 = (f32[2048]{0:T(1024)S(1)}, f32[2048]{0:T(1024)S(1)}, f32[2048]{0:T(1024)S(1)}, f32[2048]{0:T(1024)S(1)}, f32[2048]{0:T(1024)S(1)}, /*index=5*/f32[2...) fusion(f32[512]{0:T(512)S(1)} %bitcast.126, ...), kind=kLoop, calls=%fused_computation.28.clone.1 | loop fusion | flops 57640960 | bytes 161792 | tf_op jit(solution)/shard_map/while/body/eval_jaxpr/reduce_sum | solution.py:41
  182.4 0.9 fusion.56
  184.2 11.7 %fusion.58 = (f32[2048]{0:T(1024)S(1)}, f32[2048]{0:T(1024)S(1)}, f32[2048]{0:T(1024)S(1)}, f32[2048]{0:T(1024)S(1)}, f32[2048]{0:T(1024)S(1)}, /*index=5*/f32[2...) fusion(f32[512]{0:T(512)S(1)} %bitcast.126, ...), kind=kLoop, calls=%fused_computation.28.clone.1 | loop fusion | flops 57640960 | bytes 161792 | tf_op jit(solution)/shard_map/while/body/eval_jaxpr/reduce_sum | solution.py:41
  197.4 0.9 fusion.56
  199.2 11.7 %fusion.58 = (f32[2048]{0:T(1024)S(1)}, f32[2048]{0:T(1024)S(1)}, f32[2048]{0:T(1024)S(1)}, f32[2048]{0:T(1024)S(1)}, f32[2048]{0:T(1024)S(1)}, /*index=5*/f32[2...) fusion(f32[512]{0:T(512)S(1)} %bitcast.126, ...), kind=kLoop, calls=%fused_computation.28.clone.1 | loop fusion | flops 57640960 | bytes 161792 | tf_op jit(solution)/shard_map/while/body/eval_jaxpr/reduce_sum | solution.py:41
  214.3 11.7 %fusion.58 = (f32[2048]{0:T(1024)S(1)}, f32[2048]{0:T(1024)S(1)}, f32[2048]{0:T(1024)S(1)}, f32[2048]{0:T(1024)S(1)}, f32[2048]{0:T(1024)S(1)}, /*index=5*/f32[2...) fusion(f32[512]{0:T(512)S(1)} %bitcast.126, ...), kind=kLoop, calls=%fused_computation.28.clone.1 | loop fusion | flops 57640960 | bytes 161792 | tf_op jit(solution)/shard_map/while/body/eval_jaxpr/reduce_sum | solution.py:41
  229.3 11.7 %fusion.58 = (f32[2048]{0:T(1024)S(1)}, f32[2048]{0:T(1024)S(1)}, f32[2048]{0:T(1024)S(1)}, f32[2048]{0:T(1024)S(1)}, f32[2048]{0:T(1024)S(1)}, /*index=5*/f32[2...) fusion(f32[512]{0:T(512)S(1)} %bitcast.126, ...), kind=kLoop, calls=%fused_computation.28.clone.1 | loop fusion | flops 57640960 | bytes 161792 | tf_op jit(solution)/shard_map/while/body/eval_jaxpr/reduce_sum | solution.py:41
  244.3 11.7 %fusion.58 = (f32[2048]{0:T(1024)S(1)}, f32[2048]{0:T(1024)S(1)}, f32[2048]{0:T(1024)S(1)}, f32[2048]{0:T(1024)S(1)}, f32[2048]{0:T(1024)S(1)}, /*index=5*/f32[2...) fusion(f32[512]{0:T(512)S(1)} %bitcast.126, ...), kind=kLoop, calls=%fused_computation.28.clone.1 | loop fusion | flops 57640960 | bytes 161792 | tf_op jit(solution)/shard_map/while/body/eval_jaxpr/reduce_sum | solution.py:41
  259.3 11.7 %fusion.58 = (f32[2048]{0:T(1024)S(1)}, f32[2048]{0:T(1024)S(1)}, f32[2048]{0:T(1024)S(1)}, f32[2048]{0:T(1024)S(1)}, f32[2048]{0:T(1024)S(1)}, /*index=5*/f32[2...) fusion(f32[512]{0:T(512)S(1)} %bitcast.126, ...), kind=kLoop, calls=%fused_computation.28.clone.1 | loop fusion | flops 57640960 | bytes 161792 | tf_op jit(solution)/shard_map/while/body/eval_jaxpr/reduce_sum | solution.py:41
  272.2 1.0 reshape.83
  273.3 4.7 %all-to-all-start.1 = ((f32[128,1,240]{2,1,0:T(1,128)}), f32[128,1,240]{2,1,0:T(1,128)S(1)}, u32[]{:S(2)}, u32[]{:S(2)}) async-start(f32[128,1,240]{2,1,0:T(1,128)} %reshape.83), calls=%async_computation.1 | async-start | bytes 262144 | tf_op jit(solution)/shard_map/all_to_all | solution.py:129
  278.2 9.8 %all-to-all-done.1 = f32[128,1,240]{2,1,0:T(1,128)S(1)} async-done(((f32[128,1,240]{2,1,0:T(1,128)}), f32[128,1,240]{2,1,0:T(1,128)S(1)}, u32[]{:S(2)}, u32[]{:S(2)}) %all-to-all-start.1) | async-done | bytes 122912 | tf_op jit(solution)/shard_map/all_to_all | solution.py:129
  288.5 1.0 reduce
  (123 shorter events, 42.7 us)
Async XLA Ops:
  2.8 25.1 %all-to-all-start = ((f32[128,8,8]{1,2,0:T(8,128)}), f32[128,8,8]{1,2,0:T(8,128)S(1)}, u32[]{:S(2)}, u32[]{:S(2)}) async-start(f32[128,8,8]{1,2,0:T(8,128)} %broadcast_in_dim.44), calls=%async_computation | async-start | bytes 1048576 | tf_op jit(solution)/shard_map/all_to_all | solution.py:111
  273.3 14.7 %all-to-all-start.1 = ((f32[128,1,240]{2,1,0:T(1,128)}), f32[128,1,240]{2,1,0:T(1,128)S(1)}, u32[]{:S(2)}, u32[]{:S(2)}) async-start(f32[128,1,240]{2,1,0:T(1,128)} %reshape.83), calls=%async_computation.1 | async-start | bytes 262144 | tf_op jit(solution)/shard_map/all_to_all | solution.py:129

commit v3 on v2

--- a/solution.py
+++ b/solution.py
@@ -3,6 +3,8 @@
 import jax
 import jax.numpy as jnp
 from jax import lax
+from jax.experimental import pallas as pl
+from jax.experimental.pallas import tpu as pltpu
 from jax.sharding import PartitionSpec as P
 
 HIGHEST = lax.Precision.HIGHEST
@@ -41,21 +43,67 @@
     return jnp.stack([jnp.sum(term, axis=1) for term in terms_list])
 
 
+def pair_kernel(source_ref, target_ref, out_ref):
+    source_total = source_ref.shape[1]
+    target_x = target_ref[0]
+    target_y = target_ref[1]
+    target_z = target_ref[2]
+
+    def one_source(index, running):
+        delta_x = target_x - source_ref[0, index]
+        delta_y = target_y - source_ref[1, index]
+        delta_z = target_z - source_ref[2, index]
+        alpha_x = source_ref[3, index]
+        alpha_y = source_ref[4, index]
+        alpha_z = source_ref[5, index]
+        radius_sq = delta_x * delta_x + delta_y * delta_y + delta_z * delta_z + source_ref[6, index]
+        inverse = lax.rsqrt(radius_sq)
+        inverse_sq = inverse * inverse
+        kernel_three = inverse_sq * inverse
+        kernel_five = kernel_three * inverse_sq
+        cross_x = delta_y * alpha_z - delta_z * alpha_y
+        cross_y = delta_z * alpha_x - delta_x * alpha_z
+        cross_z = delta_x * alpha_y - delta_y * alpha_x
+        five_x = kernel_five * cross_x
+        five_y = kernel_five * cross_y
+        five_z = kernel_five * cross_z
+        terms = [
+            kernel_three * cross_x,
+            kernel_three * cross_y,
+            kernel_three * cross_z,
+            kernel_three * alpha_x,
+            kernel_three * alpha_y,
+            kernel_three * alpha_z,
+        ]
+        for along in (delta_x, delta_y, delta_z):
+            terms.extend([along * five_x, along * five_y, along * five_z])
+        return tuple(total + term for total, term in zip(running, terms))
+
+    start = tuple(jnp.zeros_like(target_x) for _ in range(15))
+    running = lax.fori_loop(0, source_total, one_source, start, unroll=4)
+    for row in range(15):
+        out_ref[row] = running[row]
+
+
 def pair_sums(target_pos, source_pos, source_str, source_core):
-    source_total = source_pos.shape[1]
-    block_width = math.gcd(source_total, max(512, 1048576 // target_pos.shape[1]))
-    block_steps = source_total // block_width
-
-    def one_block(running, block_index):
-        offset = block_index * block_width
-        part_pos = lax.dynamic_slice_in_dim(source_pos, offset, block_width, 1)
-        part_str = lax.dynamic_slice_in_dim(source_str, offset, block_width, 1)
-        part_core = lax.dynamic_slice_in_dim(source_core, offset, block_width, 1)
-        return (running + block_sums(target_pos, part_pos, part_str, part_core), None)
-
-    start_sums = jnp.zeros((15, target_pos.shape[1]), jnp.float32)
-    running, unused = lax.scan(one_block, start_sums, jnp.arange(block_steps, dtype=jnp.int32))
-    return running
+    target_total = target_pos.shape[1]
+    sublanes = target_total // 128
+    tile = 8 if sublanes % 8 == 0 else sublanes
+    sources = jnp.concatenate(
+        [source_pos, source_str, source_core * source_core, jnp.zeros_like(source_core)], axis=0
+    )
+    targets = target_pos.reshape(3, sublanes, 128)
+    sums = pl.pallas_call(
+        pair_kernel,
+        grid=(sublanes // tile,),
+        in_specs=[
+            pl.BlockSpec(memory_space=pltpu.SMEM),
+            pl.BlockSpec((3, tile, 128), lambda step: (0, step, 0)),
+        ],
+        out_specs=pl.BlockSpec((15, tile, 128), lambda step: (0, step, 0)),
+        out_shape=jax.ShapeDtypeStruct((15, sublanes, 128), jnp.float32),
+    )(sources, targets)
+    return sums.reshape(15, target_total)
 
 
 def combine_rows(kernel_sums):

time: 293 us -> 255 us (0.87)
  Pallas kernels: 0 us -> 202 us
  other arithmetic: 205 us -> 3.82 us
  local copies, waits for them, and re-layouts: 35 us -> 9.27 us
  loops' own time: 11.1 us -> 0 us
    pallas_call x0 -> x1, Pallas kernels: none -> 202 us  [pair_sums(): pl.pallas_call(pair_kernel, grid=(sublanes // tile,), in_specs=[pl.BlockS...]
    reduce_sum x16 -> x0, other arithmetic: 187 us -> none  [block_sums(): return jnp.stack([jnp.sum(term, axis=1) for term in terms_list])]
    slice x32 -> x0, local copies, waits for them, and re-layouts: 14.6 us -> none  [the longest x16 14.3 us: block_sums(): alpha_z = source_str[2][None, :]]
    slice x16 -> x0, other arithmetic: 14.2 us -> none  [block_sums(): delta_x = target_pos[0][:, None] - source_pos[0][None, :]]
    another operation x1 -> x0, loops' own time: 11.1 us -> none  [pair_sums(): lax.scan(one_block, start_sums, jnp.arange(block_steps, dtype=jnp.int32))]
    dynamic_slice x16 -> x0, local copies, waits for them, and re-layouts: 9.38 us -> none  [pair_sums(): lax.scan(one_block, start_sums, jnp.arange(block_steps, dtype=jnp.int32))]
where the time goes in v3:
time: 255 us; the launch traced here: 254 us
  Pallas kernels  202 us (79%)
  waiting for transfers between devices  22.4 us (9%)
  starting transfers between devices  16.1 us (6%)
  local copies, waits for them, and re-layouts  9.27 us (4%)
  other arithmetic  3.82 us (1%)
    pallas_call x1, Pallas kernels, pair_sums(): pl.pallas_call(pair_kernel, grid=(sublanes // tile,), in_specs=[pl.BlockS...  202 us
    all_to_all x1, waiting for transfers between devices, per_device(): every_cell = lax.all_to_all(copies, axes, 0, 0, tiled=True)  12.6 us
    all_to_all x1, starting transfers between devices, per_device(): every_cell = lax.all_to_all(copies, axes, 0, 0, tiled=True)  11.5 us
    all_to_all x1, waiting for transfers between devices, per_device(): lax.all_to_all(by_device, axes, 0, 0, tiled=True)  9.77 us
  transfers between devices with their start and end apart: 2, of which 2 were waited for; matrix products, arithmetic and copies ran while one was open for 0% of the time, Pallas kernels for 0%

profile of v3, /device:TPU:1, one launch (start us, length us, event | category | flops | bytes accessed | tf_op | source)
XLA Modules:
  0.0 254.4 jit_solution(2748223600130783101)
XLA Ops:
  0.6 0.0 copy-start.2
  0.7 0.7 reshape.64
  1.4 0.7 convert_bitcast_fusion
  2.1 0.8 broadcast_in_dim.44
  2.9 11.5 %all-to-all-start = ((f32[128,8,8]{1,2,0:T(8,128)}), f32[128,8,8]{1,2,0:T(8,128)S(1)}, u32[]{:S(2)}, u32[]{:S(2)}) async-start(f32[128,8,8]{1,2,0:T(8,128)} %broadcast_in_dim.44), calls=%async_computation | async-start | bytes 1048576 | tf_op jit(solution)/shard_map/all_to_all | solution.py:159
  14.5 0.1 pad.6.clone
  14.5 0.8 maximum_maximum_fusion.source_ref
  15.3 12.6 %all-to-all-done = f32[128,8,8]{1,2,0:T(8,128)S(1)} async-done(((f32[128,8,8]{1,2,0:T(8,128)}), f32[128,8,8]{1,2,0:T(8,128)S(1)}, u32[]{:S(2)}, u32[]{:S(2)}) %all-to-all-start) | async-done | bytes 32800 | tf_op jit(solution)/shard_map/all_to_all | solution.py:159
  28.0 0.1 copy.32
  28.1 0.2 reshape_reshape.9
  28.3 0.1 iota_compare_fusion
  28.4 1.0 select_reduce_fusion
  29.5 0.1 reshape.65
  29.6 0.5 copy.35
  30.1 1.4 reshape_reshape.10.target_ref
  31.5 201.9 %shard_map.77 = f32[15,16,128]{2,1,0:T(8,128)} custom-call(f32[8,8192]{1,0:T(8,128)} %maximum_maximum_fusion.source_ref, f32[3,16,128]{2,1,0:T(8,128)} %reshape_reshape.10.target_ref), custom_call_target="tpu_custom_call" | custom-call | tf_op jit(solution)/shard_map/pallas_call | solution.py:96
  233.4 1.2 reshape_reshape.11
  234.6 0.6 copy.36
  235.2 1.1 reshape.71
  236.3 4.6 %all-to-all-start.1 = ((f32[128,1,240]{2,1,0:T(1,128)}), f32[128,1,240]{2,1,0:T(1,128)S(1)}, u32[]{:S(2)}, u32[]{:S(2)}) async-start(f32[128,1,240]{2,1,0:T(1,128)} %reshape.71), calls=%async_computation.1 | async-start | bytes 262144 | tf_op jit(solution)/shard_map/all_to_all | solution.py:177
  240.9 0.1 dynamic-slice_bitcast_fusion
  241.0 0.1 compare_convert_fusion
  241.1 0.1 reshape.69
  241.1 9.8 %all-to-all-done.1 = f32[128,1,240]{2,1,0:T(1,128)S(1)} async-done(((f32[128,1,240]{2,1,0:T(1,128)}), f32[128,1,240]{2,1,0:T(1,128)S(1)}, u32[]{:S(2)}, u32[]{:S(2)}) %all-to-all-start.1) | async-done | bytes 122912 | tf_op jit(solution)/shard_map/all_to_all | solution.py:177
  250.9 0.5 broadcast.100
  251.4 1.0 reduce
  252.4 0.3 reshape.72
  252.7 0.1 reduce_sum.19
  252.9 0.1 stack.2
  253.0 0.7 copy.37
  253.6 0.1 reshape.67
  253.7 0.7 copy.38
  (18 shorter events, 0.2 us)
Async XLA Ops:
  0.6 13.8 %copy-start.2 = (f32[1,8192]{1,0:T(1,128)S(1)}, f32[1,8192]{1,0:T(1,128)}, u32[]{:S(2)}) copy-start(f32[1,8192]{1,0:T(1,128)} %param.11) | copy-start | bytes 98308
  0.6 13.9 %copy-start = (f32[3,8192]{1,0:T(4,128)S(1)}, f32[3,8192]{1,0:T(4,128)}, u32[]{:S(2)}) copy-start(f32[3,8192]{1,0:T(4,128)} %param.10) | copy-start | bytes 294916
  0.7 13.9 %copy-start.1 = (f32[3,8192]{1,0:T(4,128)S(1)}, f32[3,8192]{1,0:T(4,128)}, u32[]{:S(2)}) copy-start(f32[3,8192]{1,0:T(4,128)} %param.9) | copy-start | bytes 294916
  2.9 25.1 %all-to-all-start = ((f32[128,8,8]{1,2,0:T(8,128)}), f32[128,8,8]{1,2,0:T(8,128)S(1)}, u32[]{:S(2)}, u32[]{:S(2)}) async-start(f32[128,8,8]{1,2,0:T(8,128)} %broadcast_in_dim.44), calls=%async_computation | async-start | bytes 1048576 | tf_op jit(solution)/shard_map/all_to_all | solution.py:159
  236.3 14.6 %all-to-all-start.1 = ((f32[128,1,240]{2,1,0:T(1,128)}), f32[128,1,240]{2,1,0:T(1,128)S(1)}, u32[]{:S(2)}, u32[]{:S(2)}) async-start(f32[128,1,240]{2,1,0:T(1,128)} %reshape.71), calls=%async_computation.1 | async-start | bytes 262144 | tf_op jit(solution)/shard_map/all_to_all | solution.py:177

commit v4 on v3

--- a/solution.py
+++ b/solution.py
@@ -45,50 +45,61 @@
 
 def pair_kernel(source_ref, target_ref, out_ref):
     source_total = source_ref.shape[1]
-    target_x = target_ref[0]
-    target_y = target_ref[1]
-    target_z = target_ref[2]
+    halves = 2 if target_ref.shape[1] % 16 == 0 else 1
+    part = target_ref.shape[1] // halves
+    target_x = [target_ref[0, k * part : (k + 1) * part] for k in range(halves)]
+    target_y = [target_ref[1, k * part : (k + 1) * part] for k in range(halves)]
+    target_z = [target_ref[2, k * part : (k + 1) * part] for k in range(halves)]
 
     def one_source(index, running):
-        delta_x = target_x - source_ref[0, index]
-        delta_y = target_y - source_ref[1, index]
-        delta_z = target_z - source_ref[2, index]
+        source_x = source_ref[0, index]
+        source_y = source_ref[1, index]
+        source_z = source_ref[2, index]
         alpha_x = source_ref[3, index]
         alpha_y = source_ref[4, index]
         alpha_z = source_ref[5, index]
-        radius_sq = delta_x * delta_x + delta_y * delta_y + delta_z * delta_z + source_ref[6, index]
-        inverse = lax.rsqrt(radius_sq)
-        inverse_sq = inverse * inverse
-        kernel_three = inverse_sq * inverse
-        kernel_five = kernel_three * inverse_sq
-        cross_x = delta_y * alpha_z - delta_z * alpha_y
-        cross_y = delta_z * alpha_x - delta_x * alpha_z
-        cross_z = delta_x * alpha_y - delta_y * alpha_x
-        five_x = kernel_five * cross_x
-        five_y = kernel_five * cross_y
-        five_z = kernel_five * cross_z
-        terms = [
-            kernel_three * cross_x,
-            kernel_three * cross_y,
-            kernel_three * cross_z,
-            kernel_three * alpha_x,
-            kernel_three * alpha_y,
-            kernel_three * alpha_z,
-        ]
-        for along in (delta_x, delta_y, delta_z):
-            terms.extend([along * five_x, along * five_y, along * five_z])
-        return tuple(total + term for total, term in zip(running, terms))
-
-    start = tuple(jnp.zeros_like(target_x) for _ in range(15))
-    running = lax.fori_loop(0, source_total, one_source, start, unroll=4)
-    for row in range(15):
-        out_ref[row] = running[row]
+        core_sq = source_ref[6, index]
+        updated = []
+        for k in range(halves):
+            delta_x = target_x[k] - source_x
+            delta_y = target_y[k] - source_y
+            delta_z = target_z[k] - source_z
+            radius_sq = delta_x * delta_x + delta_y * delta_y + delta_z * delta_z + core_sq
+            inverse = lax.rsqrt(radius_sq)
+            inverse_sq = inverse * inverse
+            kernel_three = inverse_sq * inverse
+            kernel_five = kernel_three * inverse_sq
+            cross_x = delta_y * alpha_z - delta_z * alpha_y
+            cross_y = delta_z * alpha_x - delta_x * alpha_z
+            cross_z = delta_x * alpha_y - delta_y * alpha_x
+            five_x = kernel_five * cross_x
+            five_y = kernel_five * cross_y
+            five_z = kernel_five * cross_z
+            terms = [
+                kernel_three * cross_x,
+                kernel_three * cross_y,
+                kernel_three * cross_z,
+                kernel_three * alpha_x,
+                kernel_three * alpha_y,
+                kernel_three * alpha_z,
+            ]
+            for along in (delta_x, delta_y, delta_z):
+                terms.extend([along * five_x, along * five_y, along * five_z])
+            mine = running[15 * k : 15 * k + 15]
+            updated.extend(total + term for total, term in zip(mine, terms))
+        return tuple(updated)
+
+    start = tuple(jnp.zeros_like(target_x[0]) for _ in range(15 * halves))
+    running = lax.fori_loop(0, source_total, one_source, start, unroll=16)
+    for k in range(halves):
+        for row in range(15):
+            out_ref[row, k * part : (k + 1) * part] = running[15 * k + row]
 
 
 def pair_sums(target_pos, source_pos, source_str, source_core):
     target_total = target_pos.shape[1]
     sublanes = target_total // 128
-    tile = 8 if sublanes % 8 == 0 else sublanes
+    tile = 16 if sublanes % 16 == 0 else sublanes
     sources = jnp.concatenate(
         [source_pos, source_str, source_core * source_core, jnp.zeros_like(source_core)], axis=0
     )

time: 255 us -> 196 us (0.77)
  Pallas kernels: 202 us -> 144 us
    pallas_call x1, Pallas kernels: 202 us -> 144 us  [pair_sums(): pl.pallas_call(pair_kernel, grid=(sublanes // tile,), in_specs=[pl.BlockS...]
  transfers between devices with their start and end apart: 2 -> 2, of which waited for: 2 -> 2; matrix products, arithmetic and copies ran while one was open for 0% -> 1% of each run, Pallas kernels for 0% -> 0%
where the time goes in v4:
time: 196 us
  Pallas kernels  144 us (73%)
  waiting for transfers between devices  22.4 us (11%)
  starting transfers between devices  16.1 us (8%)
  local copies, waits for them, and re-layouts  9.27 us (5%)
  other arithmetic  3.82 us (2%)
    pallas_call x1, Pallas kernels, pair_sums(): pl.pallas_call(pair_kernel, grid=(sublanes // tile,), in_specs=[pl.BlockS...  144 us
    all_to_all x1, waiting for transfers between devices, per_device(): every_cell = lax.all_to_all(copies, axes, 0, 0, tiled=True)  12.6 us
    all_to_all x1, starting transfers between devices, per_device(): every_cell = lax.all_to_all(copies, axes, 0, 0, tiled=True)  11.5 us
    all_to_all x1, waiting for transfers between devices, per_device(): lax.all_to_all(by_device, axes, 0, 0, tiled=True)  9.77 us
    all_to_all x1, starting transfers between devices, per_device(): lax.all_to_all(by_device, axes, 0, 0, tiled=True)  4.64 us
  transfers between devices with their start and end apart: 2, of which 2 were waited for; matrix products, arithmetic and copies ran while one was open for 1% of the time, Pallas kernels for 0%

profile of v4, /device:TPU:1, one launch (start us, length us, event | category | flops | bytes accessed | tf_op | source)
XLA Modules:
  0.0 196.0 jit_solution(784814974917940714)
XLA Ops:
  0.6 0.0 copy-start.2
  0.7 0.7 reshape.64
  1.4 0.7 convert_bitcast_fusion
  2.1 0.8 broadcast_in_dim.44
  2.9 11.5 %all-to-all-start = ((f32[128,8,8]{1,2,0:T(8,128)}), f32[128,8,8]{1,2,0:T(8,128)S(1)}, u32[]{:S(2)}, u32[]{:S(2)}) async-start(f32[128,8,8]{1,2,0:T(8,128)} %broadcast_in_dim.44), calls=%async_computation | async-start | bytes 1048576 | tf_op jit(solution)/shard_map/all_to_all | solution.py:170
  14.5 0.1 pad.6.clone
  14.5 0.8 maximum_maximum_fusion.source_ref
  15.3 12.6 %all-to-all-done = f32[128,8,8]{1,2,0:T(8,128)S(1)} async-done(((f32[128,8,8]{1,2,0:T(8,128)}), f32[128,8,8]{1,2,0:T(8,128)S(1)}, u32[]{:S(2)}, u32[]{:S(2)}) %all-to-all-start) | async-done | bytes 32800 | tf_op jit(solution)/shard_map/all_to_all | solution.py:170
  28.0 0.1 copy.32
  28.1 0.2 reshape_reshape.9
  28.3 0.1 iota_compare_fusion
  28.4 1.0 select_reduce_fusion
  29.5 0.1 reshape.65
  29.6 0.5 copy.35
  30.1 1.4 reshape_reshape.10.target_ref
  31.5 143.6 %shard_map.77 = f32[15,16,128]{2,1,0:T(8,128)} custom-call(f32[8,8192]{1,0:T(8,128)} %maximum_maximum_fusion.source_ref, f32[3,16,128]{2,1,0:T(8,128)} %reshape_reshape.10.target_ref), custom_call_target="tpu_custom_call" | custom-call | tf_op jit(solution)/shard_map/pallas_call | solution.py:107
  175.1 1.2 reshape_reshape.11
  176.3 0.6 copy.36
  176.8 1.1 reshape.71
  177.9 4.6 %all-to-all-start.1 = ((f32[128,1,240]{2,1,0:T(1,128)}), f32[128,1,240]{2,1,0:T(1,128)S(1)}, u32[]{:S(2)}, u32[]{:S(2)}) async-start(f32[128,1,240]{2,1,0:T(1,128)} %reshape.71), calls=%async_computation.1 | async-start | bytes 262144 | tf_op jit(solution)/shard_map/all_to_all | solution.py:188
  182.6 0.1 dynamic-slice_bitcast_fusion
  182.6 0.1 compare_convert_fusion
  182.7 0.1 reshape.69
  182.8 9.8 %all-to-all-done.1 = f32[128,1,240]{2,1,0:T(1,128)S(1)} async-done(((f32[128,1,240]{2,1,0:T(1,128)}), f32[128,1,240]{2,1,0:T(1,128)S(1)}, u32[]{:S(2)}, u32[]{:S(2)}) %all-to-all-start.1) | async-done | bytes 122912 | tf_op jit(solution)/shard_map/all_to_all | solution.py:188
  192.6 0.5 broadcast.100
  193.1 1.0 reduce
  194.0 0.3 reshape.72
  194.4 0.1 reduce_sum.19
  194.5 0.1 stack.2
  194.6 0.7 copy.37
  195.3 0.1 reshape.67
  195.4 0.7 copy.38
  (18 shorter events, 0.2 us)
Async XLA Ops:
  0.6 13.8 %copy-start.2 = (f32[1,8192]{1,0:T(1,128)S(1)}, f32[1,8192]{1,0:T(1,128)}, u32[]{:S(2)}) copy-start(f32[1,8192]{1,0:T(1,128)} %param.11) | copy-start | bytes 98308
  0.6 13.9 %copy-start = (f32[3,8192]{1,0:T(4,128)S(1)}, f32[3,8192]{1,0:T(4,128)}, u32[]{:S(2)}) copy-start(f32[3,8192]{1,0:T(4,128)} %param.10) | copy-start | bytes 294916
  0.7 13.9 %copy-start.1 = (f32[3,8192]{1,0:T(4,128)S(1)}, f32[3,8192]{1,0:T(4,128)}, u32[]{:S(2)}) copy-start(f32[3,8192]{1,0:T(4,128)} %param.9) | copy-start | bytes 294916
  2.9 25.1 %all-to-all-start = ((f32[128,8,8]{1,2,0:T(8,128)}), f32[128,8,8]{1,2,0:T(8,128)S(1)}, u32[]{:S(2)}, u32[]{:S(2)}) async-start(f32[128,8,8]{1,2,0:T(8,128)} %broadcast_in_dim.44), calls=%async_computation | async-start | bytes 1048576 | tf_op jit(solution)/shard_map/all_to_all | solution.py:170
  177.9 14.6 %all-to-all-start.1 = ((f32[128,1,240]{2,1,0:T(1,128)}), f32[128,1,240]{2,1,0:T(1,128)S(1)}, u32[]{:S(2)}, u32[]{:S(2)}) async-start(f32[128,1,240]{2,1,0:T(1,128)} %reshape.71), calls=%async_computation.1 | async-start | bytes 262144 | tf_op jit(solution)/shard_map/all_to_all | solution.py:188

commit v5 on v4

--- a/solution.py
+++ b/solution.py
@@ -8,6 +8,7 @@
 from jax.sharding import PartitionSpec as P
 
 HIGHEST = lax.Precision.HIGHEST
+ROWS = 14
 
 
 def block_sums(target_pos, source_pos, source_str, source_core):
@@ -68,32 +69,33 @@
             inverse = lax.rsqrt(radius_sq)
             inverse_sq = inverse * inverse
             kernel_three = inverse_sq * inverse
-            kernel_five = kernel_three * inverse_sq
             cross_x = delta_y * alpha_z - delta_z * alpha_y
             cross_y = delta_z * alpha_x - delta_x * alpha_z
             cross_z = delta_x * alpha_y - delta_y * alpha_x
-            five_x = kernel_five * cross_x
-            five_y = kernel_five * cross_y
-            five_z = kernel_five * cross_z
+            three_x = kernel_three * cross_x
+            three_y = kernel_three * cross_y
+            three_z = kernel_three * cross_z
             terms = [
-                kernel_three * cross_x,
-                kernel_three * cross_y,
-                kernel_three * cross_z,
+                three_x,
+                three_y,
+                three_z,
                 kernel_three * alpha_x,
                 kernel_three * alpha_y,
                 kernel_three * alpha_z,
             ]
             for along in (delta_x, delta_y, delta_z):
-                terms.extend([along * five_x, along * five_y, along * five_z])
-            mine = running[15 * k : 15 * k + 15]
+                scaled = inverse_sq * along
+                terms.extend([scaled * three_x, scaled * three_y, scaled * three_z])
+            terms = terms[:ROWS]
+            mine = running[ROWS * k : ROWS * k + ROWS]
             updated.extend(total + term for total, term in zip(mine, terms))
         return tuple(updated)
 
-    start = tuple(jnp.zeros_like(target_x[0]) for _ in range(15 * halves))
-    running = lax.fori_loop(0, source_total, one_source, start, unroll=16)
+    start = tuple(jnp.zeros_like(target_x[0]) for _ in range(ROWS * halves))
+    running = lax.fori_loop(0, source_total, one_source, start, unroll=32)
     for k in range(halves):
-        for row in range(15):
-            out_ref[row, k * part : (k + 1) * part] = running[15 * k + row]
+        for row in range(ROWS):
+            out_ref[row, k * part : (k + 1) * part] = running[ROWS * k + row]
 
 
 def pair_sums(target_pos, source_pos, source_str, source_core):
@@ -111,10 +113,10 @@
             pl.BlockSpec(memory_space=pltpu.SMEM),
             pl.BlockSpec((3, tile, 128), lambda step: (0, step, 0)),
         ],
-        out_specs=pl.BlockSpec((15, tile, 128), lambda step: (0, step, 0)),
-        out_shape=jax.ShapeDtypeStruct((15, sublanes, 128), jnp.float32),
+        out_specs=pl.BlockSpec((ROWS, tile, 128), lambda step: (0, step, 0)),
+        out_shape=jax.ShapeDtypeStruct((ROWS, sublanes, 128), jnp.float32),
     )(sources, targets)
-    return sums.reshape(15, target_total)
+    return sums.reshape(ROWS, target_total)
 
 
 def combine_rows(kernel_sums):
@@ -186,6 +188,7 @@
     rows = local_sums.shape[0]
     by_device = local_sums.reshape(rows, devices, cell_total * slot_cap).transpose(1, 0, 2)
     own_rows = jnp.sum(lax.all_to_all(by_device, axes, 0, 0, tiled=True), axis=0)
+    own_rows = jnp.concatenate([own_rows, -(own_rows[6:7] + own_rows[10:11])], axis=0)
     finished_rows = combine_rows(own_rows)
     return apply_mask(finished_rows, own_counts, slot_cap)
 

time: 196 us -> 185 us (0.944)
  Pallas kernels: 144 us -> 133 us
    pallas_call x1, Pallas kernels: 144 us -> 133 us  [pair_sums(): pl.pallas_call(pair_kernel, grid=(sublanes // tile,), in_specs=[pl.BlockS...]
where the time goes in v5:
time: 185 us
  Pallas kernels  133 us (72%)
  waiting for transfers between devices  22.4 us (12%)
  starting transfers between devices  16.1 us (9%)
  local copies, waits for them, and re-layouts  9.22 us (5%)
  other arithmetic  3.82 us (2%)
    pallas_call x1, Pallas kernels, pair_sums(): pl.pallas_call(pair_kernel, grid=(sublanes // tile,), in_specs=[pl.BlockS...  133 us
    all_to_all x1, waiting for transfers between devices, per_device(): every_cell = lax.all_to_all(copies, axes, 0, 0, tiled=True)  12.6 us
    all_to_all x1, starting transfers between devices, per_device(): every_cell = lax.all_to_all(copies, axes, 0, 0, tiled=True)  11.5 us
    all_to_all x1, waiting for transfers between devices, per_device(): lax.all_to_all(by_device, axes, 0, 0, tiled=True)  9.77 us
    all_to_all x1, starting transfers between devices, per_device(): lax.all_to_all(by_device, axes, 0, 0, tiled=True)  4.64 us
  transfers between devices with their start and end apart: 2, of which 2 were waited for; matrix products, arithmetic and copies ran while one was open for 1% of the time, Pallas kernels for 0%

profile of v5, /device:TPU:1, one launch (start us, length us, event | category | flops | bytes accessed | tf_op | source)
XLA Modules:
  0.0 184.9 jit_solution(5512877389328490872)
XLA Ops:
  0.6 0.0 copy-start.2
  0.7 0.7 reshape.64
  1.4 0.7 convert_bitcast_fusion
  2.1 0.8 broadcast_in_dim.44
  2.9 11.5 %all-to-all-start = ((f32[128,8,8]{1,2,0:T(8,128)}), f32[128,8,8]{1,2,0:T(8,128)S(1)}, u32[]{:S(2)}, u32[]{:S(2)}) async-start(f32[128,8,8]{1,2,0:T(8,128)} %broadcast_in_dim.44), calls=%async_computation | async-start | bytes 1048576 | tf_op jit(solution)/shard_map/all_to_all | solution.py:172
  14.5 0.1 pad.6.clone
  14.5 0.8 maximum_maximum_fusion.source_ref
  15.3 12.6 %all-to-all-done = f32[128,8,8]{1,2,0:T(8,128)S(1)} async-done(((f32[128,8,8]{1,2,0:T(8,128)}), f32[128,8,8]{1,2,0:T(8,128)S(1)}, u32[]{:S(2)}, u32[]{:S(2)}) %all-to-all-start) | async-done | bytes 32800 | tf_op jit(solution)/shard_map/all_to_all | solution.py:172
  28.0 0.1 copy.32
  28.1 0.2 reshape_reshape.9
  28.3 0.1 iota_compare_fusion
  28.4 1.0 select_reduce_fusion
  29.5 0.1 reshape.65
  29.6 0.5 copy.35
  30.1 1.4 reshape_reshape.10.target_ref
  31.5 132.5 %shard_map.77 = f32[14,16,128]{2,1,0:T(8,128)} custom-call(f32[8,8192]{1,0:T(8,128)} %maximum_maximum_fusion.source_ref, f32[3,16,128]{2,1,0:T(8,128)} %reshape_reshape.10.target_ref), custom_call_target="tpu_custom_call" | custom-call | tf_op jit(solution)/shard_map/pallas_call | solution.py:109
  164.0 1.2 reshape_reshape.11
  165.2 0.5 copy.36
  165.7 1.1 reshape.71
  166.8 4.6 %all-to-all-start.1 = ((f32[128,1,224]{2,1,0:T(1,128)}), f32[128,1,224]{2,1,0:T(1,128)S(1)}, u32[]{:S(2)}, u32[]{:S(2)}) async-start(f32[128,1,224]{2,1,0:T(1,128)} %reshape.71), calls=%async_computation.1 | async-start | bytes 262144 | tf_op jit(solution)/shard_map/all_to_all | solution.py:190
  171.5 0.1 dynamic-slice_bitcast_fusion
  171.5 0.1 compare_convert_fusion
  171.6 0.1 reshape.69
  171.7 9.8 %all-to-all-done.1 = f32[128,1,224]{2,1,0:T(1,128)S(1)} async-done(((f32[128,1,224]{2,1,0:T(1,128)}), f32[128,1,224]{2,1,0:T(1,128)S(1)}, u32[]{:S(2)}, u32[]{:S(2)}) %all-to-all-start.1) | async-done | bytes 114720 | tf_op jit(solution)/shard_map/all_to_all | solution.py:190
  181.5 0.5 broadcast.100
  182.0 1.0 reduce
  182.9 0.3 reshape.72
  183.3 0.1 reduce_sum.19
  183.4 0.1 stack.2
  183.5 0.7 copy.37
  184.2 0.1 reshape.67
  184.3 0.7 copy.38
  (18 shorter events, 0.2 us)
Async XLA Ops:
  0.6 13.8 %copy-start.2 = (f32[1,8192]{1,0:T(1,128)S(1)}, f32[1,8192]{1,0:T(1,128)}, u32[]{:S(2)}) copy-start(f32[1,8192]{1,0:T(1,128)} %param.11) | copy-start | bytes 98308
  0.6 13.9 %copy-start = (f32[3,8192]{1,0:T(4,128)S(1)}, f32[3,8192]{1,0:T(4,128)}, u32[]{:S(2)}) copy-start(f32[3,8192]{1,0:T(4,128)} %param.10) | copy-start | bytes 294916
  0.7 13.9 %copy-start.1 = (f32[3,8192]{1,0:T(4,128)S(1)}, f32[3,8192]{1,0:T(4,128)}, u32[]{:S(2)}) copy-start(f32[3,8192]{1,0:T(4,128)} %param.9) | copy-start | bytes 294916
  2.9 25.1 %all-to-all-start = ((f32[128,8,8]{1,2,0:T(8,128)}), f32[128,8,8]{1,2,0:T(8,128)S(1)}, u32[]{:S(2)}, u32[]{:S(2)}) async-start(f32[128,8,8]{1,2,0:T(8,128)} %broadcast_in_dim.44), calls=%async_computation | async-start | bytes 1048576 | tf_op jit(solution)/shard_map/all_to_all | solution.py:172
  166.8 14.6 %all-to-all-start.1 = ((f32[128,1,224]{2,1,0:T(1,128)}), f32[128,1,224]{2,1,0:T(1,128)S(1)}, u32[]{:S(2)}, u32[]{:S(2)}) async-start(f32[128,1,224]{2,1,0:T(1,128)} %reshape.71), calls=%async_computation.1 | async-start | bytes 262144 | tf_op jit(solution)/shard_map/all_to_all | solution.py:190

commit v6 on v5

--- a/solution.py
+++ b/solution.py
@@ -69,20 +69,13 @@
             inverse = lax.rsqrt(radius_sq)
             inverse_sq = inverse * inverse
             kernel_three = inverse_sq * inverse
-            cross_x = delta_y * alpha_z - delta_z * alpha_y
-            cross_y = delta_z * alpha_x - delta_x * alpha_z
-            cross_z = delta_x * alpha_y - delta_y * alpha_x
-            three_x = kernel_three * cross_x
-            three_y = kernel_three * cross_y
-            three_z = kernel_three * cross_z
-            terms = [
-                three_x,
-                three_y,
-                three_z,
-                kernel_three * alpha_x,
-                kernel_three * alpha_y,
-                kernel_three * alpha_z,
-            ]
+            swirl_x = kernel_three * alpha_x
+            swirl_y = kernel_three * alpha_y
+            swirl_z = kernel_three * alpha_z
+            three_x = delta_y * swirl_z - delta_z * swirl_y
+            three_y = delta_z * swirl_x - delta_x * swirl_z
+            three_z = delta_x * swirl_y - delta_y * swirl_x
+            terms = [three_x, three_y, three_z, swirl_x, swirl_y, swirl_z]
             for along in (delta_x, delta_y, delta_z):
                 scaled = inverse_sq * along
                 terms.extend([scaled * three_x, scaled * three_y, scaled * three_z])

time: 185 us -> 182 us (0.984)
  Pallas kernels: 133 us -> 129 us
    pallas_call x1, Pallas kernels: 133 us -> 129 us  [pair_sums(): pl.pallas_call(pair_kernel, grid=(sublanes // tile,), in_specs=[pl.BlockS...]
where the time goes in v6:
time: 182 us; the launch traced here: 181 us
  Pallas kernels  129 us (71%)
  waiting for transfers between devices  22.4 us (12%)
  starting transfers between devices  16.1 us (9%)
  local copies, waits for them, and re-layouts  9.22 us (5%)
  other arithmetic  3.82 us (2%)
    pallas_call x1, Pallas kernels, pair_sums(): pl.pallas_call(pair_kernel, grid=(sublanes // tile,), in_specs=[pl.BlockS...  129 us
    all_to_all x1, waiting for transfers between devices, per_device(): every_cell = lax.all_to_all(copies, axes, 0, 0, tiled=True)  12.6 us
    all_to_all x1, starting transfers between devices, per_device(): every_cell = lax.all_to_all(copies, axes, 0, 0, tiled=True)  11.5 us
    all_to_all x1, waiting for transfers between devices, per_device(): lax.all_to_all(by_device, axes, 0, 0, tiled=True)  9.77 us
    all_to_all x1, starting transfers between devices, per_device(): lax.all_to_all(by_device, axes, 0, 0, tiled=True)  4.64 us
  transfers between devices with their start and end apart: 2, of which 2 were waited for; matrix products, arithmetic and copies ran while one was open for 1% of the time, Pallas kernels for 0%

profile of v6, /device:TPU:1, one launch (start us, length us, event | category | flops | bytes accessed | tf_op | source)
XLA Modules:
  0.0 181.4 jit_solution(18311624727781600219)
XLA Ops:
  0.6 0.0 copy-start.2
  0.7 0.7 reshape.64
  1.4 0.7 convert_bitcast_fusion
  2.1 0.8 broadcast_in_dim.44
  2.9 11.5 %all-to-all-start = ((f32[128,8,8]{1,2,0:T(8,128)}), f32[128,8,8]{1,2,0:T(8,128)S(1)}, u32[]{:S(2)}, u32[]{:S(2)}) async-start(f32[128,8,8]{1,2,0:T(8,128)} %broadcast_in_dim.44), calls=%async_computation | async-start | bytes 1048576 | tf_op jit(solution)/shard_map/all_to_all | solution.py:165
  14.5 0.1 pad.6.clone
  14.5 0.8 maximum_maximum_fusion.source_ref
  15.3 12.6 %all-to-all-done = f32[128,8,8]{1,2,0:T(8,128)S(1)} async-done(((f32[128,8,8]{1,2,0:T(8,128)}), f32[128,8,8]{1,2,0:T(8,128)S(1)}, u32[]{:S(2)}, u32[]{:S(2)}) %all-to-all-start) | async-done | bytes 32800 | tf_op jit(solution)/shard_map/all_to_all | solution.py:165
  28.0 0.1 copy.32
  28.1 0.2 reshape_reshape.9
  28.3 0.1 iota_compare_fusion
  28.4 1.0 select_reduce_fusion
  29.5 0.1 reshape.65
  29.6 0.5 copy.35
  30.1 1.4 reshape_reshape.10.target_ref
  31.5 129.0 %shard_map.77 = f32[14,16,128]{2,1,0:T(8,128)} custom-call(f32[8,8192]{1,0:T(8,128)} %maximum_maximum_fusion.source_ref, f32[3,16,128]{2,1,0:T(8,128)} %reshape_reshape.10.target_ref), custom_call_target="tpu_custom_call" | custom-call | tf_op jit(solution)/shard_map/pallas_call | solution.py:102
  160.5 1.2 reshape_reshape.11
  161.7 0.5 copy.36
  162.2 1.1 reshape.71
  163.3 4.6 %all-to-all-start.1 = ((f32[128,1,224]{2,1,0:T(1,128)}), f32[128,1,224]{2,1,0:T(1,128)S(1)}, u32[]{:S(2)}, u32[]{:S(2)}) async-start(f32[128,1,224]{2,1,0:T(1,128)} %reshape.71), calls=%async_computation.1 | async-start | bytes 262144 | tf_op jit(solution)/shard_map/all_to_all | solution.py:183
  168.0 0.1 dynamic-slice_bitcast_fusion
  168.0 0.1 compare_convert_fusion
  168.1 0.1 reshape.69
  168.2 9.8 %all-to-all-done.1 = f32[128,1,224]{2,1,0:T(1,128)S(1)} async-done(((f32[128,1,224]{2,1,0:T(1,128)}), f32[128,1,224]{2,1,0:T(1,128)S(1)}, u32[]{:S(2)}, u32[]{:S(2)}) %all-to-all-start.1) | async-done | bytes 114720 | tf_op jit(solution)/shard_map/all_to_all | solution.py:183
  178.0 0.5 broadcast.100
  178.5 1.0 reduce
  179.4 0.3 reshape.72
  179.7 0.1 reduce_sum.19
  179.9 0.1 stack.2
  180.0 0.7 copy.37
  180.7 0.1 reshape.67
  180.8 0.7 copy.38
  (18 shorter events, 0.2 us)
Async XLA Ops:
  0.6 13.8 %copy-start.2 = (f32[1,8192]{1,0:T(1,128)S(1)}, f32[1,8192]{1,0:T(1,128)}, u32[]{:S(2)}) copy-start(f32[1,8192]{1,0:T(1,128)} %param.11) | copy-start | bytes 98308
  0.6 13.9 %copy-start = (f32[3,8192]{1,0:T(4,128)S(1)}, f32[3,8192]{1,0:T(4,128)}, u32[]{:S(2)}) copy-start(f32[3,8192]{1,0:T(4,128)} %param.10) | copy-start | bytes 294916
  0.7 13.9 %copy-start.1 = (f32[3,8192]{1,0:T(4,128)S(1)}, f32[3,8192]{1,0:T(4,128)}, u32[]{:S(2)}) copy-start(f32[3,8192]{1,0:T(4,128)} %param.9) | copy-start | bytes 294916
  2.9 25.1 %all-to-all-start = ((f32[128,8,8]{1,2,0:T(8,128)}), f32[128,8,8]{1,2,0:T(8,128)S(1)}, u32[]{:S(2)}, u32[]{:S(2)}) async-start(f32[128,8,8]{1,2,0:T(8,128)} %broadcast_in_dim.44), calls=%async_computation | async-start | bytes 1048576 | tf_op jit(solution)/shard_map/all_to_all | solution.py:165
  163.3 14.6 %all-to-all-start.1 = ((f32[128,1,224]{2,1,0:T(1,128)}), f32[128,1,224]{2,1,0:T(1,128)S(1)}, u32[]{:S(2)}, u32[]{:S(2)}) async-start(f32[128,1,224]{2,1,0:T(1,128)} %reshape.71), calls=%async_computation.1 | async-start | bytes 262144 | tf_op jit(solution)/shard_map/all_to_all | solution.py:183

commit v7 on v6

--- a/solution.py
+++ b/solution.py
@@ -161,7 +161,8 @@
         axis=1,
     )
     devices = lax.axis_size("row") * col_devs
-    copies = jnp.broadcast_to(packed[None], (devices,) + packed.shape)
+    flat = packed.reshape(1, 1, packed.size)
+    copies = jnp.broadcast_to(flat, (devices, 1, packed.size))
     every_cell = lax.all_to_all(copies, axes, 0, 0, tiled=True)
     all_cells = devices * cell_total
     every_cell = every_cell.reshape(all_cells, packed.shape[1])

time: 182 us -> 179 us (0.984)
  waiting for transfers between devices: 22.4 us -> 16.8 us
  other arithmetic: 3.82 us -> 6.96 us
    all_to_all x1, waiting for transfers between devices: 12.6 us -> 6.99 us  [per_device(): every_cell = lax.all_to_all(copies, axes, 0, 0, tiled=True)]
  transfers between devices with their start and end apart: 2 -> 2, of which waited for: 2 -> 2; matrix products, arithmetic and copies ran while one was open for 1% -> 2% of each run, Pallas kernels for 0% -> 0%
where the time goes in v7:
time: 179 us
  Pallas kernels  129 us (72%)
  waiting for transfers between devices  16.8 us (9%)
  starting transfers between devices  15.8 us (9%)
  local copies, waits for them, and re-layouts  9.73 us (5%)
  other arithmetic  6.96 us (4%)
    pallas_call x1, Pallas kernels, pair_sums(): pl.pallas_call(pair_kernel, grid=(sublanes // tile,), in_specs=[pl.BlockS...  129 us
    all_to_all x1, starting transfers between devices, per_device(): every_cell = lax.all_to_all(copies, axes, 0, 0, tiled=True)  11.5 us
    all_to_all x1, waiting for transfers between devices, per_device(): lax.all_to_all(by_device, axes, 0, 0, tiled=True)  9.77 us
    all_to_all x1, waiting for transfers between devices, per_device(): every_cell = lax.all_to_all(copies, axes, 0, 0, tiled=True)  6.99 us
    all_to_all x1, starting transfers between devices, per_device(): lax.all_to_all(by_device, axes, 0, 0, tiled=True)  4.26 us
  transfers between devices with their start and end apart: 2, of which 2 were waited for; matrix products, arithmetic and copies ran while one was open for 2% of the time, Pallas kernels for 0%

profile of v7, /device:TPU:1, one launch (start us, length us, event | category | flops | bytes accessed | tf_op | source)
XLA Modules:
  0.0 179.0 jit_solution(11118586947635559807)
XLA Ops:
  0.6 0.7 reshape.67
  1.3 0.7 convert_bitcast_fusion
  2.1 0.1 broadcast_in_dim.45
  2.2 0.7 broadcast_in_dim.46
  2.8 11.5 %all-to-all-start = ((f32[128,1,64]{2,1,0:T(1,128)}), f32[128,1,64]{2,1,0:T(1,128)S(1)}, u32[]{:S(2)}, u32[]{:S(2)}) async-start(f32[128,1,64]{2,1,0:T(1,128)} %broadcast_in_dim.46), calls=%async_computation | async-start | bytes 131072 | tf_op jit(solution)/shard_map/all_to_all | solution.py:166
  14.3 0.9 mul.101
  15.3 1.8 maximum_maximum_fusion.source_ref
  17.0 7.0 %all-to-all-done = f32[128,1,64]{2,1,0:T(1,128)S(1)} async-done(((f32[128,1,64]{2,1,0:T(1,128)}), f32[128,1,64]{2,1,0:T(1,128)S(1)}, u32[]{:S(2)}, u32[]{:S(2)}) %all-to-all-start) | async-done | bytes 32800 | tf_op jit(solution)/shard_map/all_to_all | solution.py:166
  24.0 0.5 broadcast.104
  24.5 0.8 reduce.5
  25.4 0.2 reshape_reshape.9
  25.5 0.5 fusion
  26.1 0.2 copy.28
  26.3 0.1 iota_compare_fusion
  26.4 1.0 select_reduce_fusion
  27.4 0.1 reshape.68
  27.6 0.5 copy.30
  28.1 1.4 reshape_reshape.10.target_ref
  29.5 129.0 %shard_map.77 = f32[14,16,128]{2,1,0:T(8,128)} custom-call(f32[8,8192]{1,0:T(8,128)} %maximum_maximum_fusion.source_ref, f32[3,16,128]{2,1,0:T(8,128)} %reshape_reshape.10.target_ref), custom_call_target="tpu_custom_call" | custom-call | tf_op jit(solution)/shard_map/pallas_call | solution.py:102
  158.5 1.2 reshape_reshape.11
  159.7 0.5 copy.31
  160.2 1.1 reshape.84
  161.3 4.3 %all-to-all-start.1 = ((f32[128,1,224]{2,1,0:T(1,128)}), f32[128,1,224]{2,1,0:T(1,128)S(1)}, u32[]{:S(2)}, u32[]{:S(2)}) async-start(f32[128,1,224]{2,1,0:T(1,128)} %reshape.84), calls=%async_computation.1 | async-start | bytes 262144 | tf_op jit(solution)/shard_map/all_to_all | solution.py:184
  165.6 0.1 dynamic-slice_bitcast_fusion
  165.7 0.1 reshape.72
  165.8 9.8 %all-to-all-done.1 = f32[128,1,224]{2,1,0:T(1,128)S(1)} async-done(((f32[128,1,224]{2,1,0:T(1,128)}), f32[128,1,224]{2,1,0:T(1,128)S(1)}, u32[]{:S(2)}, u32[]{:S(2)}) %all-to-all-start.1) | async-done | bytes 114720 | tf_op jit(solution)/shard_map/all_to_all | solution.py:184
  175.6 0.5 broadcast.105
  176.1 1.0 reduce.6
  177.0 0.3 reshape.85
  177.3 0.1 reduce_sum.19
  177.6 0.7 copy.32
  178.4 0.7 copy.33
  (15 shorter events, 0.4 us)
Async XLA Ops:
  2.8 21.2 %all-to-all-start = ((f32[128,1,64]{2,1,0:T(1,128)}), f32[128,1,64]{2,1,0:T(1,128)S(1)}, u32[]{:S(2)}, u32[]{:S(2)}) async-start(f32[128,1,64]{2,1,0:T(1,128)} %broadcast_in_dim.46), calls=%async_computation | async-start | bytes 131072 | tf_op jit(solution)/shard_map/all_to_all | solution.py:166
  161.3 14.3 %all-to-all-start.1 = ((f32[128,1,224]{2,1,0:T(1,128)}), f32[128,1,224]{2,1,0:T(1,128)S(1)}, u32[]{:S(2)}, u32[]{:S(2)}) async-start(f32[128,1,224]{2,1,0:T(1,128)} %reshape.84), calls=%async_computation.1 | async-start | bytes 262144 | tf_op jit(solution)/shard_map/all_to_all | solution.py:184

commit v8 on v7

--- a/solution.py
+++ b/solution.py
@@ -46,7 +46,7 @@
 
 def pair_kernel(source_ref, target_ref, out_ref):
     source_total = source_ref.shape[1]
-    halves = 2 if target_ref.shape[1] % 16 == 0 else 1
+    halves = 1
     part = target_ref.shape[1] // halves
     target_x = [target_ref[0, k * part : (k + 1) * part] for k in range(halves)]
     target_y = [target_ref[1, k * part : (k + 1) * part] for k in range(halves)]
@@ -169,15 +169,23 @@
     groups = all_cells // group_cells
     grouped = every_cell.reshape(groups, group_cells, 3 * slot_cap + 2)
     within = grouped[:, :, -1].astype(jnp.int32) % group_cells
-    position = jnp.arange(group_cells, dtype=jnp.int32)
-    chosen = within[:, None, :] == position[None, :, None]
-    relaid = jnp.sum(
-        jnp.where(chosen[:, :, :, None], grouped[:, None, :, : 3 * slot_cap + 1], 0.0), axis=2
-    ).reshape(all_cells, 3 * slot_cap + 1)
-    target_pos = relaid[:, : 3 * slot_cap].reshape(all_cells, 3, slot_cap)
-    target_pos = target_pos.transpose(1, 0, 2).reshape(3, all_cells * slot_cap)
+    lane = jnp.arange(group_cells * slot_cap, dtype=jnp.int32)
+    chosen = within[:, None, :] == (lane // slot_cap)[None, :, None]
+    coords = grouped[:, :, : 3 * slot_cap].reshape(groups, group_cells, 3, slot_cap)
+    picked = coords[..., 0][..., None]
+    for slot in range(1, slot_cap):
+        picked = jnp.where((lane % slot_cap) == slot, coords[..., slot][..., None], picked)
+    picked = picked.transpose(2, 0, 3, 1)
+    target_pos = jnp.sum(jnp.where(chosen[None], picked, 0.0), axis=-1)
+    target_pos = target_pos.reshape(3, all_cells * slot_cap)
     device = lax.axis_index("row") * col_devs + lax.axis_index("col")
-    own_counts = lax.dynamic_slice_in_dim(relaid[:, 3 * slot_cap], device * cell_total, cell_total)
+    own_group = lax.dynamic_index_in_dim(grouped, device // col_devs, 0, keepdims=False)
+    own_within = lax.dynamic_index_in_dim(within, device // col_devs, 0, keepdims=False)
+    own_slots = (device % col_devs) * cell_total + jnp.arange(cell_total, dtype=jnp.int32)
+    own_counts = jnp.sum(
+        jnp.where(own_within[None, :] == own_slots[:, None], own_group[None, :, 3 * slot_cap], 0.0),
+        axis=1,
+    )
     local_sums = pair_sums(target_pos, wake_pos, wake_strength, wake_core)
     rows = local_sums.shape[0]
     by_device = local_sums.reshape(rows, devices, cell_total * slot_cap).transpose(1, 0, 2)

time: 179 us -> 177 us (0.989)
  local copies, waits for them, and re-layouts: 9.73 us -> 7.75 us
where the time goes in v8:
time: 177 us
  Pallas kernels  128 us (72%)
  waiting for transfers between devices  16.6 us (9%)
  starting transfers between devices  15.8 us (9%)
  other arithmetic  7.85 us (4%)
  local copies, waits for them, and re-layouts  7.75 us (4%)
    pallas_call x1, Pallas kernels, pair_sums(): pl.pallas_call(pair_kernel, grid=(sublanes // tile,), in_specs=[pl.BlockS...  128 us
    all_to_all x1, starting transfers between devices, per_device(): every_cell = lax.all_to_all(copies, axes, 0, 0, tiled=True)  11.5 us
    all_to_all x1, waiting for transfers between devices, per_device(): lax.all_to_all(by_device, axes, 0, 0, tiled=True)  9.67 us
    all_to_all x1, waiting for transfers between devices, per_device(): every_cell = lax.all_to_all(copies, axes, 0, 0, tiled=True)  6.94 us
    all_to_all x1, starting transfers between devices, per_device(): lax.all_to_all(by_device, axes, 0, 0, tiled=True)  4.26 us
  transfers between devices with their start and end apart: 2, of which 2 were waited for; matrix products, arithmetic and copies ran while one was open for 2% of the time, Pallas kernels for 0%

profile of v8, /device:TPU:1, one launch (start us, length us, event | category | flops | bytes accessed | tf_op | source)
XLA Modules:
  0.0 176.9 jit_solution(5348084831811858876)
XLA Ops:
  0.6 0.7 reshape.78
  1.3 0.7 convert_bitcast_fusion
  2.1 0.1 broadcast_in_dim.80
  2.2 0.7 broadcast_in_dim.81
  2.8 11.5 %all-to-all-start = ((f32[128,1,64]{2,1,0:T(1,128)}), f32[128,1,64]{2,1,0:T(1,128)S(1)}, u32[]{:S(2)}, u32[]{:S(2)}) async-start(f32[128,1,64]{2,1,0:T(1,128)} %broadcast_in_dim.81), calls=%async_computation | async-start | bytes 131072 | tf_op jit(solution)/shard_map/all_to_all | solution.py:166
  14.4 0.9 mul.101
  15.3 0.1 pad.6.clone
  15.3 1.8 maximum_maximum_fusion.source_ref
  17.1 6.9 %all-to-all-done = f32[128,1,64]{2,1,0:T(1,128)S(1)} async-done(((f32[128,1,64]{2,1,0:T(1,128)}), f32[128,1,64]{2,1,0:T(1,128)S(1)}, u32[]{:S(2)}, u32[]{:S(2)}) %all-to-all-start) | async-done | bytes 32800 | tf_op jit(solution)/shard_map/all_to_all | solution.py:166
  24.0 0.5 broadcast.156
  24.5 0.8 reduce.5
  25.4 0.2 reshape_reshape.6
  25.5 0.5 fusion
  26.2 0.2 copy.28
  26.4 0.2 broadcast_compare_fusion
  26.6 1.6 select_reduce_fusion.target_ref
  28.2 128.1 %shard_map.77 = f32[14,16,128]{2,1,0:T(8,128)} custom-call(f32[8,8192]{1,0:T(8,128)} %maximum_maximum_fusion.source_ref, f32[3,16,128]{2,1,0:T(8,128)} %select_reduce_fusion.target_ref), custom_call_target="tpu_custom_call" | custom-call | tf_op jit(solution)/shard_map/pallas_call | solution.py:102
  156.3 1.2 reshape_reshape.7
  157.5 0.5 copy.29
  158.1 1.1 reshape.94
  159.1 4.3 %all-to-all-start.1 = ((f32[128,1,224]{2,1,0:T(1,128)}), f32[128,1,224]{2,1,0:T(1,128)S(1)}, u32[]{:S(2)}, u32[]{:S(2)}) async-start(f32[128,1,224]{2,1,0:T(1,128)} %reshape.94), calls=%async_computation.1 | async-start | bytes 262144 | tf_op jit(solution)/shard_map/all_to_all | solution.py:192
  163.4 0.2 select_reduce_fusion.1
  163.6 0.1 compare_convert_fusion
  163.7 0.1 reshape.82
  163.7 9.7 %all-to-all-done.1 = f32[128,1,224]{2,1,0:T(1,128)S(1)} async-done(((f32[128,1,224]{2,1,0:T(1,128)}), f32[128,1,224]{2,1,0:T(1,128)S(1)}, u32[]{:S(2)}, u32[]{:S(2)}) %all-to-all-start.1) | async-done | bytes 114720 | tf_op jit(solution)/shard_map/all_to_all | solution.py:192
  173.4 0.5 broadcast.157
  173.9 1.0 reduce.6
  174.9 0.3 reshape.95
  175.2 0.1 reduce_sum.28
  175.4 0.7 copy.31
  176.1 0.1 reshape.80
  176.2 0.7 copy.32
  (17 shorter events, 0.3 us)
Async XLA Ops:
  2.8 21.2 %all-to-all-start = ((f32[128,1,64]{2,1,0:T(1,128)}), f32[128,1,64]{2,1,0:T(1,128)S(1)}, u32[]{:S(2)}, u32[]{:S(2)}) async-start(f32[128,1,64]{2,1,0:T(1,128)} %broadcast_in_dim.81), calls=%async_computation | async-start | bytes 131072 | tf_op jit(solution)/shard_map/all_to_all | solution.py:166
  159.1 14.3 %all-to-all-start.1 = ((f32[128,1,224]{2,1,0:T(1,128)}), f32[128,1,224]{2,1,0:T(1,128)S(1)}, u32[]{:S(2)}, u32[]{:S(2)}) async-start(f32[128,1,224]{2,1,0:T(1,128)} %reshape.94), calls=%async_computation.1 | async-start | bytes 262144 | tf_op jit(solution)/shard_map/all_to_all | solution.py:192

commit v9 on v8

--- a/solution.py
+++ b/solution.py
@@ -45,68 +45,67 @@
 
 
 def pair_kernel(source_ref, target_ref, out_ref):
-    source_total = source_ref.shape[1]
-    halves = 1
-    part = target_ref.shape[1] // halves
-    target_x = [target_ref[0, k * part : (k + 1) * part] for k in range(halves)]
-    target_y = [target_ref[1, k * part : (k + 1) * part] for k in range(halves)]
-    target_z = [target_ref[2, k * part : (k + 1) * part] for k in range(halves)]
+    chunk = source_ref.shape[1]
+    shape = target_ref.shape[1:]
+    target_x = target_ref[0]
+    target_y = target_ref[1]
+    target_z = target_ref[2]
+
+    @pl.when(pl.program_id(0) == 0)
+    def _():
+        out_ref[...] = jnp.zeros_like(out_ref)
 
     def one_source(index, running):
-        source_x = source_ref[0, index]
-        source_y = source_ref[1, index]
-        source_z = source_ref[2, index]
-        alpha_x = source_ref[3, index]
-        alpha_y = source_ref[4, index]
-        alpha_z = source_ref[5, index]
-        core_sq = source_ref[6, index]
-        updated = []
-        for k in range(halves):
-            delta_x = target_x[k] - source_x
-            delta_y = target_y[k] - source_y
-            delta_z = target_z[k] - source_z
-            radius_sq = delta_x * delta_x + delta_y * delta_y + delta_z * delta_z + core_sq
-            inverse = lax.rsqrt(radius_sq)
-            inverse_sq = inverse * inverse
-            kernel_three = inverse_sq * inverse
-            swirl_x = kernel_three * alpha_x
-            swirl_y = kernel_three * alpha_y
-            swirl_z = kernel_three * alpha_z
-            three_x = delta_y * swirl_z - delta_z * swirl_y
-            three_y = delta_z * swirl_x - delta_x * swirl_z
-            three_z = delta_x * swirl_y - delta_y * swirl_x
-            terms = [three_x, three_y, three_z, swirl_x, swirl_y, swirl_z]
-            for along in (delta_x, delta_y, delta_z):
-                scaled = inverse_sq * along
-                terms.extend([scaled * three_x, scaled * three_y, scaled * three_z])
-            terms = terms[:ROWS]
-            mine = running[ROWS * k : ROWS * k + ROWS]
-            updated.extend(total + term for total, term in zip(mine, terms))
-        return tuple(updated)
-
-    start = tuple(jnp.zeros_like(target_x[0]) for _ in range(ROWS * halves))
-    running = lax.fori_loop(0, source_total, one_source, start, unroll=32)
-    for k in range(halves):
-        for row in range(ROWS):
-            out_ref[row, k * part : (k + 1) * part] = running[ROWS * k + row]
-
-
-def pair_sums(target_pos, source_pos, source_str, source_core):
+        def spread(row):
+            return jnp.broadcast_to(source_ref[row, pl.ds(index, 1), :], shape)
+
+        delta_x = target_x - spread(0)
+        delta_y = target_y - spread(1)
+        delta_z = target_z - spread(2)
+        alpha_x = spread(3)
+        alpha_y = spread(4)
+        alpha_z = spread(5)
+        radius_sq = delta_x * delta_x + delta_y * delta_y + delta_z * delta_z + spread(6)
+        inverse = lax.rsqrt(radius_sq)
+        inverse_sq = inverse * inverse
+        kernel_three = inverse_sq * inverse
+        swirl_x = kernel_three * alpha_x
+        swirl_y = kernel_three * alpha_y
+        swirl_z = kernel_three * alpha_z
+        three_x = delta_y * swirl_z - delta_z * swirl_y
+        three_y = delta_z * swirl_x - delta_x * swirl_z
+        three_z = delta_x * swirl_y - delta_y * swirl_x
+        terms = [three_x, three_y, three_z, swirl_x, swirl_y, swirl_z]
+        for along in (delta_x, delta_y, delta_z):
+            scaled = inverse_sq * along
+            terms.extend([scaled * three_x, scaled * three_y, scaled * three_z])
+        return tuple(total + term for total, term in zip(running, terms[:ROWS]))
+
+    start = tuple(out_ref[row] for row in range(ROWS))
+    running = lax.fori_loop(0, chunk, one_source, start, unroll=32)
+    for row in range(ROWS):
+        out_ref[row] = running[row]
+
+
+def spread_sources(source_pos, source_str, source_core):
+    sources = jnp.concatenate([source_pos, source_str, source_core * source_core], axis=0)
+    return jnp.broadcast_to(sources[:, :, None], sources.shape + (128,))
+
+
+def pair_sums(target_pos, sources):
     target_total = target_pos.shape[1]
+    source_total = sources.shape[1]
     sublanes = target_total // 128
-    tile = 16 if sublanes % 16 == 0 else sublanes
-    sources = jnp.concatenate(
-        [source_pos, source_str, source_core * source_core, jnp.zeros_like(source_core)], axis=0
-    )
+    chunk = math.gcd(source_total, 1024)
     targets = target_pos.reshape(3, sublanes, 128)
     sums = pl.pallas_call(
         pair_kernel,
-        grid=(sublanes // tile,),
+        grid=(source_total // chunk,),
         in_specs=[
-            pl.BlockSpec(memory_space=pltpu.SMEM),
-            pl.BlockSpec((3, tile, 128), lambda step: (0, step, 0)),
+            pl.BlockSpec((7, chunk, 128), lambda step: (0, step, 0)),
+            pl.BlockSpec((3, sublanes, 128), lambda step: (0, 0, 0)),
         ],
-        out_specs=pl.BlockSpec((ROWS, tile, 128), lambda step: (0, step, 0)),
+        out_specs=pl.BlockSpec((ROWS, sublanes, 128), lambda step: (0, 0, 0)),
         out_shape=jax.ShapeDtypeStruct((ROWS, sublanes, 128), jnp.float32),
     )(sources, targets)
     return sums.reshape(ROWS, target_total)
@@ -163,6 +162,8 @@
     devices = lax.axis_size("row") * col_devs
     flat = packed.reshape(1, 1, packed.size)
     copies = jnp.broadcast_to(flat, (devices, 1, packed.size))
+    sources = spread_sources(wake_pos, wake_strength, wake_core)
+    copies, sources = lax.optimization_barrier((copies, sources))
     every_cell = lax.all_to_all(copies, axes, 0, 0, tiled=True)
     all_cells = devices * cell_total
     every_cell = every_cell.reshape(all_cells, packed.shape[1])
@@ -186,7 +187,7 @@
         jnp.where(own_within[None, :] == own_slots[:, None], own_group[None, :, 3 * slot_cap], 0.0),
         axis=1,
     )
-    local_sums = pair_sums(target_pos, wake_pos, wake_strength, wake_core)
+    local_sums = pair_sums(target_pos, sources)
     rows = local_sums.shape[0]
     by_device = local_sums.reshape(rows, devices, cell_total * slot_cap).transpose(1, 0, 2)
     own_rows = jnp.sum(lax.all_to_all(by_device, axes, 0, 0, tiled=True), axis=0)

time: 177 us -> 177 us (level)
  Pallas kernels: 128 us -> 116 us
  local copies, waits for them, and re-layouts: 7.75 us -> 17.7 us
  waiting for transfers between devices: 16.6 us -> 19.3 us
    pallas_call x1, Pallas kernels: 128 us -> 116 us  [pair_sums(): pl.pallas_call(pair_kernel, grid=(source_total // chunk,), in_specs=[pl.B...]
    broadcast_in_dim x0 -> x1, local copies, waits for them, and re-layouts: none -> 10 us  [spread_sources(): return jnp.broadcast_to(sources[:, :, None], sources.shape + (128,))]
    all_to_all x1, waiting for transfers between devices: 6.94 us -> 9.6 us  [per_device(): every_cell = lax.all_to_all(copies, axes, 0, 0, tiled=True)]
  transfers between devices with their start and end apart: 2 -> 2, of which waited for: 2 -> 2; matrix products, arithmetic and copies ran while one was open for 2% -> 0% of each run, Pallas kernels for 0% -> 0%
where the time goes in v9:
time: 177 us; the launch traced here: 176 us
  Pallas kernels  116 us (66%)
  waiting for transfers between devices  19.3 us (11%)
  local copies, waits for them, and re-layouts  17.7 us (10%)
  starting transfers between devices  15.8 us (9%)
  other arithmetic  7.15 us (4%)
    pallas_call x1, Pallas kernels, pair_sums(): pl.pallas_call(pair_kernel, grid=(source_total // chunk,), in_specs=[pl.B...  116 us
    all_to_all x1, starting transfers between devices, per_device(): every_cell = lax.all_to_all(copies, axes, 0, 0, tiled=True)  11.5 us
    broadcast_in_dim x1, local copies, waits for them, and re-layouts, spread_sources(): return jnp.broadcast_to(sources[:, :, None], sources.shape + (128,))  10 us
    all_to_all x1, waiting for transfers between devices, per_device(): lax.all_to_all(by_device, axes, 0, 0, tiled=True)  9.67 us
    all_to_all x1, waiting for transfers between devices, per_device(): every_cell = lax.all_to_all(copies, axes, 0, 0, tiled=True)  9.6 us
    all_to_all x1, starting transfers between devices, per_device(): lax.all_to_all(by_device, axes, 0, 0, tiled=True)  4.28 us
  transfers between devices with their start and end apart: 2, of which 2 were waited for; matrix products, arithmetic and copies ran while one was open for 0% of the time, Pallas kernels for 0%

profile of v9, /device:TPU:1, one launch (start us, length us, event | category | flops | bytes accessed | tf_op | source)
XLA Modules:
  0.0 176.4 jit_solution(17864265939204848627)
XLA Ops:
  0.6 0.7 reshape.79
  1.3 0.7 convert_bitcast_fusion
  2.1 0.1 broadcast_in_dim.82
  2.2 0.9 mul.101
  3.0 1.1 pad_maximum_fusion
  4.1 0.7 broadcast_in_dim.83
  4.8 10.0 %broadcast_in_dim.84.source_ref = f32[7,8192,128]{2,1,0:T(8,128)} broadcast(f32[7,8192]{1,0:T(8,128)S(1)} %pad_maximum_fusion), dimensions={0,1} | broadcast | bytes 29589504 | tf_op jit(solution)/shard_map/broadcast_in_dim | solution.py:92
  14.8 11.5 %all-to-all-start = ((f32[128,1,64]{2,1,0:T(1,128)}), f32[128,1,64]{2,1,0:T(1,128)S(1)}, u32[]{:S(2)}, u32[]{:S(2)}) async-start(f32[128,1,64]{2,1,0:T(1,128)} %broadcast_in_dim.83), calls=%async_computation | async-start | bytes 131072 | tf_op jit(solution)/shard_map/all_to_all | solution.py:167
  26.4 9.6 %all-to-all-done = f32[128,1,64]{2,1,0:T(1,128)S(1)} async-done(((f32[128,1,64]{2,1,0:T(1,128)}), f32[128,1,64]{2,1,0:T(1,128)S(1)}, u32[]{:S(2)}, u32[]{:S(2)}) %all-to-all-start) | async-done | bytes 32800 | tf_op jit(solution)/shard_map/all_to_all | solution.py:167
  36.0 0.5 broadcast.155
  36.5 0.8 reduce.5
  37.3 0.2 reshape_reshape.6
  37.5 0.5 fusion
  38.1 0.2 copy.28
  38.4 0.2 broadcast_compare_fusion
  38.6 1.6 select_reduce_fusion.target_ref
  40.2 115.7 %shard_map.77 = f32[14,16,128]{2,1,0:T(8,128)} custom-call(f32[7,8192,128]{2,1,0:T(8,128)} %broadcast_in_dim.84.source_ref, f32[3,16,128]{2,1,0:T(8,128)} %select_reduce_fusion.target_ref), custom_call_target="tpu_custom_call" | custom-call | tf_op jit(solution)/shard_map/pallas_call | solution.py:101
  155.9 1.2 reshape_reshape.7
  157.1 0.5 copy.29
  157.6 1.1 reshape.94
  158.7 4.3 %all-to-all-start.1 = ((f32[128,1,224]{2,1,0:T(1,128)}), f32[128,1,224]{2,1,0:T(1,128)S(1)}, u32[]{:S(2)}, u32[]{:S(2)}) async-start(f32[128,1,224]{2,1,0:T(1,128)} %reshape.94), calls=%async_computation.1 | async-start | bytes 262144 | tf_op jit(solution)/shard_map/all_to_all | solution.py:193
  163.0 0.2 select_reduce_fusion.1
  163.2 0.1 compare_convert_fusion
  163.2 0.1 reshape.83
  163.3 9.7 %all-to-all-done.1 = f32[128,1,224]{2,1,0:T(1,128)S(1)} async-done(((f32[128,1,224]{2,1,0:T(1,128)}), f32[128,1,224]{2,1,0:T(1,128)S(1)}, u32[]{:S(2)}, u32[]{:S(2)}) %all-to-all-start.1) | async-done | bytes 114720 | tf_op jit(solution)/shard_map/all_to_all | solution.py:193
  173.0 0.5 broadcast.156
  173.5 1.0 reduce.6
  174.5 0.3 reshape.95
  174.8 0.1 reduce_sum.28
  175.0 0.7 copy.31
  175.7 0.1 reshape.81
  175.8 0.7 copy.32
  (17 shorter events, 0.3 us)
Async XLA Ops:
  14.8 21.2 %all-to-all-start = ((f32[128,1,64]{2,1,0:T(1,128)}), f32[128,1,64]{2,1,0:T(1,128)S(1)}, u32[]{:S(2)}, u32[]{:S(2)}) async-start(f32[128,1,64]{2,1,0:T(1,128)} %broadcast_in_dim.83), calls=%async_computation | async-start | bytes 131072 | tf_op jit(solution)/shard_map/all_to_all | solution.py:167
  158.7 14.3 %all-to-all-start.1 = ((f32[128,1,224]{2,1,0:T(1,128)}), f32[128,1,224]{2,1,0:T(1,128)S(1)}, u32[]{:S(2)}, u32[]{:S(2)}) async-start(f32[128,1,224]{2,1,0:T(1,128)} %reshape.94), calls=%async_computation.1 | async-start | bytes 262144 | tf_op jit(solution)/shard_map/all_to_all | solution.py:193

commit v10 on v9

--- a/solution.py
+++ b/solution.py
@@ -163,8 +163,8 @@
     flat = packed.reshape(1, 1, packed.size)
     copies = jnp.broadcast_to(flat, (devices, 1, packed.size))
     sources = spread_sources(wake_pos, wake_strength, wake_core)
-    copies, sources = lax.optimization_barrier((copies, sources))
     every_cell = lax.all_to_all(copies, axes, 0, 0, tiled=True)
+    every_cell, sources = lax.optimization_barrier((every_cell, sources))
     all_cells = devices * cell_total
     every_cell = every_cell.reshape(all_cells, packed.shape[1])
     groups = all_cells // group_cells

time: 177 us -> 175 us (0.989)
  waiting for transfers between devices: 19.3 us -> 17.3 us
    all_to_all x1, waiting for transfers between devices: 9.6 us -> 7.67 us  [per_device(): every_cell = lax.all_to_all(copies, axes, 0, 0, tiled=True)]
  transfers between devices with their start and end apart: 2 -> 2, of which waited for: 2 -> 2; matrix products, arithmetic and copies ran while one was open for 0% -> 1% of each run, Pallas kernels for 0% -> 0%
where the time goes in v10:
time: 175 us
  Pallas kernels  116 us (66%)
  local copies, waits for them, and re-layouts  17.7 us (10%)
  waiting for transfers between devices  17.3 us (10%)
  starting transfers between devices  15.8 us (9%)
  other arithmetic  7.15 us (4%)
    pallas_call x1, Pallas kernels, pair_sums(): pl.pallas_call(pair_kernel, grid=(source_total // chunk,), in_specs=[pl.B...  116 us
    all_to_all x1, starting transfers between devices, per_device(): every_cell = lax.all_to_all(copies, axes, 0, 0, tiled=True)  11.5 us
    broadcast_in_dim x1, local copies, waits for them, and re-layouts, spread_sources(): return jnp.broadcast_to(sources[:, :, None], sources.shape + (128,))  10 us
    all_to_all x1, waiting for transfers between devices, per_device(): lax.all_to_all(by_device, axes, 0, 0, tiled=True)  9.67 us
    all_to_all x1, waiting for transfers between devices, per_device(): every_cell = lax.all_to_all(copies, axes, 0, 0, tiled=True)  7.67 us
    all_to_all x1, starting transfers between devices, per_device(): lax.all_to_all(by_device, axes, 0, 0, tiled=True)  4.26 us
  transfers between devices with their start and end apart: 2, of which 2 were waited for; matrix products, arithmetic and copies ran while one was open for 1% of the time, Pallas kernels for 0%

profile of v10, /device:TPU:1, one launch (start us, length us, event | category | flops | bytes accessed | tf_op | source)
XLA Modules:
  0.0 174.5 jit_solution(9258530298501957926)
XLA Ops:
  0.6 0.7 reshape.79
  1.3 0.7 convert_bitcast_fusion
  2.1 0.1 broadcast_in_dim.82
  2.2 0.7 broadcast_in_dim.83
  2.8 11.5 %all-to-all-start = ((f32[128,1,64]{2,1,0:T(1,128)}), f32[128,1,64]{2,1,0:T(1,128)S(1)}, u32[]{:S(2)}, u32[]{:S(2)}) async-start(f32[128,1,64]{2,1,0:T(1,128)} %broadcast_in_dim.83), calls=%async_computation | async-start | bytes 131072 | tf_op jit(solution)/shard_map/all_to_all | solution.py:166
  14.4 0.9 mul.101
  15.3 1.1 pad_maximum_fusion
  16.4 7.7 %all-to-all-done = f32[128,1,64]{2,1,0:T(1,128)S(1)} async-done(((f32[128,1,64]{2,1,0:T(1,128)}), f32[128,1,64]{2,1,0:T(1,128)S(1)}, u32[]{:S(2)}, u32[]{:S(2)}) %all-to-all-start) | async-done | bytes 32800 | tf_op jit(solution)/shard_map/all_to_all | solution.py:166
  24.0 10.0 %broadcast_in_dim.84.source_ref = f32[7,8192,128]{2,1,0:T(8,128)} broadcast(f32[7,8192]{1,0:T(8,128)S(1)} %pad_maximum_fusion), dimensions={0,1} | broadcast | bytes 29589504 | tf_op jit(solution)/shard_map/broadcast_in_dim | solution.py:92
  34.1 0.5 broadcast.155
  34.6 0.8 reduce.5
  35.4 0.2 reshape_reshape.6
  35.6 0.5 fusion
  36.2 0.2 copy.28
  36.5 0.2 broadcast_compare_fusion
  36.7 1.6 select_reduce_fusion.target_ref
  38.3 115.7 %shard_map.77 = f32[14,16,128]{2,1,0:T(8,128)} custom-call(f32[7,8192,128]{2,1,0:T(8,128)} %broadcast_in_dim.84.source_ref, f32[3,16,128]{2,1,0:T(8,128)} %select_reduce_fusion.target_ref), custom_call_target="tpu_custom_call" | custom-call | tf_op jit(solution)/shard_map/pallas_call | solution.py:101
  154.0 1.2 reshape_reshape.7
  155.2 0.5 copy.29
  155.7 1.1 reshape.94
  156.8 4.3 %all-to-all-start.1 = ((f32[128,1,224]{2,1,0:T(1,128)}), f32[128,1,224]{2,1,0:T(1,128)S(1)}, u32[]{:S(2)}, u32[]{:S(2)}) async-start(f32[128,1,224]{2,1,0:T(1,128)} %reshape.94), calls=%async_computation.1 | async-start | bytes 262144 | tf_op jit(solution)/shard_map/all_to_all | solution.py:193
  161.0 0.2 select_reduce_fusion.1
  161.2 0.1 compare_convert_fusion
  161.3 0.1 reshape.83
  161.4 9.7 %all-to-all-done.1 = f32[128,1,224]{2,1,0:T(1,128)S(1)} async-done(((f32[128,1,224]{2,1,0:T(1,128)}), f32[128,1,224]{2,1,0:T(1,128)S(1)}, u32[]{:S(2)}, u32[]{:S(2)}) %all-to-all-start.1) | async-done | bytes 114720 | tf_op jit(solution)/shard_map/all_to_all | solution.py:193
  171.1 0.5 broadcast.156
  171.6 1.0 reduce.6
  172.5 0.3 reshape.95
  172.8 0.1 reduce_sum.28
  173.1 0.7 copy.31
  173.8 0.1 reshape.81
  173.8 0.7 copy.32
  (17 shorter events, 0.3 us)
Async XLA Ops:
  2.8 21.2 %all-to-all-start = ((f32[128,1,64]{2,1,0:T(1,128)}), f32[128,1,64]{2,1,0:T(1,128)S(1)}, u32[]{:S(2)}, u32[]{:S(2)}) async-start(f32[128,1,64]{2,1,0:T(1,128)} %broadcast_in_dim.83), calls=%async_computation | async-start | bytes 131072 | tf_op jit(solution)/shard_map/all_to_all | solution.py:166
  156.8 14.3 %all-to-all-start.1 = ((f32[128,1,224]{2,1,0:T(1,128)}), f32[128,1,224]{2,1,0:T(1,128)S(1)}, u32[]{:S(2)}, u32[]{:S(2)}) async-start(f32[128,1,224]{2,1,0:T(1,128)} %reshape.94), calls=%async_computation.1 | async-start | bytes 262144 | tf_op jit(solution)/shard_map/all_to_all | solution.py:193

commit v11 on v10

--- a/solution.py
+++ b/solution.py
@@ -44,7 +44,7 @@
     return jnp.stack([jnp.sum(term, axis=1) for term in terms_list])
 
 
-def pair_kernel(source_ref, target_ref, out_ref):
+def pair_kernel(source_ref, target_ref, out_ref, total_ref):
     chunk = source_ref.shape[1]
     shape = target_ref.shape[1:]
     target_x = target_ref[0]
@@ -53,7 +53,7 @@
 
     @pl.when(pl.program_id(0) == 0)
     def _():
-        out_ref[...] = jnp.zeros_like(out_ref)
+        total_ref[...] = jnp.zeros_like(total_ref)
 
     def one_source(index, running):
         def spread(row):
@@ -81,10 +81,16 @@
             terms.extend([scaled * three_x, scaled * three_y, scaled * three_z])
         return tuple(total + term for total, term in zip(running, terms[:ROWS]))
 
-    start = tuple(out_ref[row] for row in range(ROWS))
+    start = tuple(total_ref[row] for row in range(ROWS))
     running = lax.fori_loop(0, chunk, one_source, start, unroll=32)
     for row in range(ROWS):
-        out_ref[row] = running[row]
+        total_ref[row] = running[row]
+
+    @pl.when(pl.program_id(0) == pl.num_programs(0) - 1)
+    def _():
+        width = shape[0]
+        for row in range(ROWS):
+            out_ref[:, 0, row * width : (row + 1) * width] = running[row].T
 
 
 def spread_sources(source_pos, source_str, source_core):
@@ -92,23 +98,21 @@
     return jnp.broadcast_to(sources[:, :, None], sources.shape + (128,))
 
 
-def pair_sums(target_pos, sources):
-    target_total = target_pos.shape[1]
+def pair_sums(targets, sources):
+    per_device, devices = targets.shape[1:]
     source_total = sources.shape[1]
-    sublanes = target_total // 128
     chunk = math.gcd(source_total, 1024)
-    targets = target_pos.reshape(3, sublanes, 128)
-    sums = pl.pallas_call(
+    return pl.pallas_call(
         pair_kernel,
         grid=(source_total // chunk,),
         in_specs=[
             pl.BlockSpec((7, chunk, 128), lambda step: (0, step, 0)),
-            pl.BlockSpec((3, sublanes, 128), lambda step: (0, 0, 0)),
+            pl.BlockSpec((3, per_device, devices), lambda step: (0, 0, 0)),
         ],
-        out_specs=pl.BlockSpec((ROWS, sublanes, 128), lambda step: (0, 0, 0)),
-        out_shape=jax.ShapeDtypeStruct((ROWS, sublanes, 128), jnp.float32),
+        out_specs=pl.BlockSpec((devices, 1, ROWS * per_device), lambda step: (0, 0, 0)),
+        out_shape=jax.ShapeDtypeStruct((devices, 1, ROWS * per_device), jnp.float32),
+        scratch_shapes=[pltpu.VMEM((ROWS, per_device, devices), jnp.float32)],
     )(sources, targets)
-    return sums.reshape(ROWS, target_total)
 
 
 def combine_rows(kernel_sums):
@@ -170,15 +174,18 @@
     groups = all_cells // group_cells
     grouped = every_cell.reshape(groups, group_cells, 3 * slot_cap + 2)
     within = grouped[:, :, -1].astype(jnp.int32) % group_cells
-    lane = jnp.arange(group_cells * slot_cap, dtype=jnp.int32)
-    chosen = within[:, None, :] == (lane // slot_cap)[None, :, None]
     coords = grouped[:, :, : 3 * slot_cap].reshape(groups, group_cells, 3, slot_cap)
-    picked = coords[..., 0][..., None]
+    per_device = cell_total * slot_cap
+    index = jnp.arange(per_device, dtype=jnp.int32)[:, None]
+    peer = jnp.arange(devices, dtype=jnp.int32)[None, :]
+    wanted = (peer % col_devs) * cell_total + index // slot_cap
+    within_peer = jnp.repeat(within, col_devs, axis=0)
+    chosen = within_peer[None, :, :] == wanted[:, :, None]
+    coords_peer = jnp.repeat(coords, col_devs, axis=0).transpose(2, 3, 0, 1)
+    picked = coords_peer[:, 0][:, None]
     for slot in range(1, slot_cap):
-        picked = jnp.where((lane % slot_cap) == slot, coords[..., slot][..., None], picked)
-    picked = picked.transpose(2, 0, 3, 1)
+        picked = jnp.where((index % slot_cap == slot)[None, :, :, None], coords_peer[:, slot][:, None], picked)
     target_pos = jnp.sum(jnp.where(chosen[None], picked, 0.0), axis=-1)
-    target_pos = target_pos.reshape(3, all_cells * slot_cap)
     device = lax.axis_index("row") * col_devs + lax.axis_index("col")
     own_group = lax.dynamic_index_in_dim(grouped, device // col_devs, 0, keepdims=False)
     own_within = lax.dynamic_index_in_dim(within, device // col_devs, 0, keepdims=False)
@@ -187,10 +194,9 @@
         jnp.where(own_within[None, :] == own_slots[:, None], own_group[None, :, 3 * slot_cap], 0.0),
         axis=1,
     )
-    local_sums = pair_sums(target_pos, sources)
-    rows = local_sums.shape[0]
-    by_device = local_sums.reshape(rows, devices, cell_total * slot_cap).transpose(1, 0, 2)
+    by_device = pair_sums(target_pos, sources)
     own_rows = jnp.sum(lax.all_to_all(by_device, axes, 0, 0, tiled=True), axis=0)
+    own_rows = own_rows.reshape(ROWS, per_device)
     own_rows = jnp.concatenate([own_rows, -(own_rows[6:7] + own_rows[10:11])], axis=0)
     finished_rows = combine_rows(own_rows)
     return apply_mask(finished_rows, own_counts, slot_cap)

time: 175 us -> 173 us (0.989)
  local copies, waits for them, and re-layouts: 17.7 us -> 14.5 us
  Pallas kernels: 116 us -> 119 us
    pallas_call x1, Pallas kernels: 116 us -> 119 us  [pair_sums(): pl.pallas_call(pair_kernel, grid=(source_total // chunk,), in_specs=[pl.B...]
where the time goes in v11:
time: 173 us; the launch traced here: 172 us
  Pallas kernels  119 us (69%)
  waiting for transfers between devices  17.3 us (10%)
  starting transfers between devices  15.7 us (9%)
  local copies, waits for them, and re-layouts  14.5 us (8%)
  other arithmetic  5.6 us (3%)
    pallas_call x1, Pallas kernels, pair_sums(): pl.pallas_call(pair_kernel, grid=(source_total // chunk,), in_specs=[pl.B...  119 us
    all_to_all x1, starting transfers between devices, per_device(): every_cell = lax.all_to_all(copies, axes, 0, 0, tiled=True)  11.5 us
    broadcast_in_dim x1, local copies, waits for them, and re-layouts, spread_sources(): return jnp.broadcast_to(sources[:, :, None], sources.shape + (128,))  10 us
    all_to_all x1, waiting for transfers between devices, per_device(): lax.all_to_all(by_device, axes, 0, 0, tiled=True)  9.67 us
    all_to_all x1, waiting for transfers between devices, per_device(): every_cell = lax.all_to_all(copies, axes, 0, 0, tiled=True)  7.59 us
    all_to_all x1, starting transfers between devices, per_device(): lax.all_to_all(by_device, axes, 0, 0, tiled=True)  4.25 us
  transfers between devices with their start and end apart: 2, of which 2 were waited for; matrix products, arithmetic and copies ran while one was open for 1% of the time, Pallas kernels for 0%

profile of v11, /device:TPU:1, one launch (start us, length us, event | category | flops | bytes accessed | tf_op | source)
XLA Modules:
  0.0 172.4 jit_solution(5041724239894542077)
XLA Ops:
  0.6 0.7 reshape.183
  1.3 0.7 convert_bitcast_fusion
  2.0 0.1 copy.35
  2.1 0.1 broadcast_in_dim.90
  2.2 0.7 broadcast_in_dim.91
  2.8 11.5 %all-to-all-start = ((f32[128,1,64]{2,1,0:T(1,128)}), f32[128,1,64]{2,1,0:T(1,128)S(1)}, u32[]{:S(2)}, u32[]{:S(2)}) async-start(f32[128,1,64]{2,1,0:T(1,128)} %broadcast_in_dim.91), calls=%async_computation | async-start | bytes 131072 | tf_op jit(solution)/shard_map/all_to_all | solution.py:170
  14.4 0.9 mul.110
  15.3 0.1 broadcast_add_fusion
  15.3 1.1 pad_maximum_fusion
  16.4 7.6 %all-to-all-done = f32[128,1,64]{2,1,0:T(1,128)S(1)} async-done(((f32[128,1,64]{2,1,0:T(1,128)}), f32[128,1,64]{2,1,0:T(1,128)S(1)}, u32[]{:S(2)}, u32[]{:S(2)}) %all-to-all-start) | async-done | bytes 32800 | tf_op jit(solution)/shard_map/all_to_all | solution.py:170
  24.0 10.0 %broadcast_in_dim.92.source_ref = f32[7,8192,128]{2,1,0:T(8,128)} broadcast(f32[7,8192]{1,0:T(8,128)S(1)} %pad_maximum_fusion), dimensions={0,1} | broadcast | bytes 29589504 | tf_op jit(solution)/shard_map/broadcast_in_dim | solution.py:98
  34.1 0.5 broadcast.221
  34.6 0.8 reduce.6
  35.4 0.2 reshape_reshape.3
  35.6 0.5 fusion
  36.2 0.2 copy.37
  36.5 0.1 copy.38
  36.7 0.1 copy.39
  36.8 0.1 copy.36
  36.8 0.1 broadcast_compare_fusion
  36.9 1.0 select_reduce_fusion.target_ref
  37.9 118.5 %shard_map.77 = f32[128,1,224]{2,1,0:T(1,128)} custom-call(f32[7,8192,128]{2,1,0:T(8,128)} %broadcast_in_dim.92.source_ref, f32[3,16,128]{2,1,0:T(8,128)} %select_reduce_fusion.target_ref), custom_call_target="tpu_custom_call" | custom-call | tf_op jit(solution)/shard_map/pallas_call | solution.py:105
  156.4 4.2 %all-to-all-start.1 = ((f32[128,1,224]{2,1,0:T(1,128)}), f32[128,1,224]{2,1,0:T(1,128)S(1)}, u32[]{:S(2)}, u32[]{:S(2)}) async-start(f32[128,1,224]{2,1,0:T(1,128)} %shard_map.77), calls=%async_computation.1 | async-start | bytes 262144 | tf_op jit(solution)/shard_map/all_to_all | solution.py:198
  160.7 0.2 select_reduce_fusion.1
  160.9 0.1 compare_convert_fusion
  160.9 0.1 reshape.188
  161.0 9.7 %all-to-all-done.1 = f32[128,1,224]{2,1,0:T(1,128)S(1)} async-done(((f32[128,1,224]{2,1,0:T(1,128)}), f32[128,1,224]{2,1,0:T(1,128)S(1)}, u32[]{:S(2)}, u32[]{:S(2)}) %all-to-all-start.1) | async-done | bytes 114720 | tf_op jit(solution)/shard_map/all_to_all | solution.py:198
  170.7 0.2 reduce_sum.30
  170.8 0.1 subtract_multiply_fusion
  171.0 0.1 reshape.186
  171.1 0.7 copy.42
  171.8 0.7 copy.41
  (18 shorter events, 0.3 us)
Async XLA Ops:
  2.8 21.2 %all-to-all-start = ((f32[128,1,64]{2,1,0:T(1,128)}), f32[128,1,64]{2,1,0:T(1,128)S(1)}, u32[]{:S(2)}, u32[]{:S(2)}) async-start(f32[128,1,64]{2,1,0:T(1,128)} %broadcast_in_dim.91), calls=%async_computation | async-start | bytes 131072 | tf_op jit(solution)/shard_map/all_to_all | solution.py:170
  156.4 14.3 %all-to-all-start.1 = ((f32[128,1,224]{2,1,0:T(1,128)}), f32[128,1,224]{2,1,0:T(1,128)S(1)}, u32[]{:S(2)}, u32[]{:S(2)}) async-start(f32[128,1,224]{2,1,0:T(1,128)} %shard_map.77), calls=%async_computation.1 | async-start | bytes 262144 | tf_op jit(solution)/shard_map/all_to_all | solution.py:198

commit v12 on v11

--- a/solution.py
+++ b/solution.py
@@ -178,13 +178,13 @@
     per_device = cell_total * slot_cap
     index = jnp.arange(per_device, dtype=jnp.int32)[:, None]
     peer = jnp.arange(devices, dtype=jnp.int32)[None, :]
-    wanted = (peer % col_devs) * cell_total + index // slot_cap
+    wanted = (peer % col_devs) * cell_total + index % cell_total
     within_peer = jnp.repeat(within, col_devs, axis=0)
     chosen = within_peer[None, :, :] == wanted[:, :, None]
     coords_peer = jnp.repeat(coords, col_devs, axis=0).transpose(2, 3, 0, 1)
     picked = coords_peer[:, 0][:, None]
     for slot in range(1, slot_cap):
-        picked = jnp.where((index % slot_cap == slot)[None, :, :, None], coords_peer[:, slot][:, None], picked)
+        picked = jnp.where((index // cell_total == slot)[None, :, :, None], coords_peer[:, slot][:, None], picked)
     target_pos = jnp.sum(jnp.where(chosen[None], picked, 0.0), axis=-1)
     device = lax.axis_index("row") * col_devs + lax.axis_index("col")
     own_group = lax.dynamic_index_in_dim(grouped, device // col_devs, 0, keepdims=False)
@@ -199,7 +199,11 @@
     own_rows = own_rows.reshape(ROWS, per_device)
     own_rows = jnp.concatenate([own_rows, -(own_rows[6:7] + own_rows[10:11])], axis=0)
     finished_rows = combine_rows(own_rows)
-    return apply_mask(finished_rows, own_counts, slot_cap)
+    slot_ids = jnp.arange(slot_cap).astype(own_counts.dtype)
+    alive = (slot_ids[:, None] < own_counts[None, :]).astype(jnp.float32)
+    velocity = (finished_rows[0:3].reshape(3, slot_cap, cell_total) * alive[None]).transpose(0, 2, 1)
+    gradient = (finished_rows[3:12].reshape(9, slot_cap, cell_total) * alive[None]).transpose(0, 2, 1)
+    return velocity, gradient
 
 
 def solution(mesh):

time: 173 us -> 173 us (level)
  no operation moved by 1% of the time
where the time goes in v12:
time: 173 us; the launch traced here: 172 us
  Pallas kernels  119 us (69%)
  waiting for transfers between devices  17.3 us (10%)
  starting transfers between devices  15.7 us (9%)
  local copies, waits for them, and re-layouts  13.7 us (8%)
  other arithmetic  6.24 us (4%)
    pallas_call x1, Pallas kernels, pair_sums(): pl.pallas_call(pair_kernel, grid=(source_total // chunk,), in_specs=[pl.B...  119 us
    all_to_all x1, starting transfers between devices, per_device(): every_cell = lax.all_to_all(copies, axes, 0, 0, tiled=True)  11.5 us
    broadcast_in_dim x1, local copies, waits for them, and re-layouts, spread_sources(): return jnp.broadcast_to(sources[:, :, None], sources.shape + (128,))  10 us
    all_to_all x1, waiting for transfers between devices, per_device(): lax.all_to_all(by_device, axes, 0, 0, tiled=True)  9.75 us
    all_to_all x1, waiting for transfers between devices, per_device(): every_cell = lax.all_to_all(copies, axes, 0, 0, tiled=True)  7.59 us
    all_to_all x1, starting transfers between devices, per_device(): lax.all_to_all(by_device, axes, 0, 0, tiled=True)  4.25 us
  transfers between devices with their start and end apart: 2, of which 2 were waited for; matrix products, arithmetic and copies ran while one was open for 1% of the time, Pallas kernels for 0%

profile of v12, /device:TPU:1, one launch (start us, length us, event | category | flops | bytes accessed | tf_op | source)
XLA Modules:
  0.0 172.4 jit_solution(208997950991521958)
XLA Ops:
  0.6 0.7 reshape.194
  1.3 0.7 convert_bitcast_fusion
  2.0 0.1 copy.34
  2.1 0.1 broadcast_in_dim.92
  2.2 0.7 broadcast_in_dim.93
  2.8 11.5 %all-to-all-start = ((f32[128,1,64]{2,1,0:T(1,128)}), f32[128,1,64]{2,1,0:T(1,128)S(1)}, u32[]{:S(2)}, u32[]{:S(2)}) async-start(f32[128,1,64]{2,1,0:T(1,128)} %broadcast_in_dim.93), calls=%async_computation | async-start | bytes 131072 | tf_op jit(solution)/shard_map/all_to_all | solution.py:170
  14.4 0.9 mul.118
  15.3 0.1 broadcast_add_fusion
  15.3 1.1 pad_maximum_fusion
  16.4 7.6 %all-to-all-done = f32[128,1,64]{2,1,0:T(1,128)S(1)} async-done(((f32[128,1,64]{2,1,0:T(1,128)}), f32[128,1,64]{2,1,0:T(1,128)S(1)}, u32[]{:S(2)}, u32[]{:S(2)}) %all-to-all-start) | async-done | bytes 32800 | tf_op jit(solution)/shard_map/all_to_all | solution.py:170
  24.0 10.0 %broadcast_in_dim.94.source_ref = f32[7,8192,128]{2,1,0:T(8,128)} broadcast(f32[7,8192]{1,0:T(8,128)S(1)} %pad_maximum_fusion), dimensions={0,1} | broadcast | bytes 29589504 | tf_op jit(solution)/shard_map/broadcast_in_dim | solution.py:98
  34.1 0.5 broadcast.238
  34.6 0.8 reduce.6
  35.4 0.2 reshape_reshape.3
  35.6 0.5 fusion
  36.2 0.2 copy.36
  36.5 0.1 copy.35
  36.6 0.1 copy.37
  36.7 0.1 copy.38
  36.9 0.1 broadcast_compare_fusion
  36.9 1.0 select_reduce_fusion.target_ref
  37.9 118.5 %shard_map.77 = f32[128,1,224]{2,1,0:T(1,128)} custom-call(f32[7,8192,128]{2,1,0:T(8,128)} %broadcast_in_dim.94.source_ref, f32[3,16,128]{2,1,0:T(8,128)} %select_reduce_fusion.target_ref), custom_call_target="tpu_custom_call" | custom-call | tf_op jit(solution)/shard_map/pallas_call | solution.py:105
  156.4 4.2 %all-to-all-start.1 = ((f32[128,1,224]{2,1,0:T(1,128)}), f32[128,1,224]{2,1,0:T(1,128)S(1)}, u32[]{:S(2)}, u32[]{:S(2)}) async-start(f32[128,1,224]{2,1,0:T(1,128)} %shard_map.77), calls=%async_computation.1 | async-start | bytes 262144 | tf_op jit(solution)/shard_map/all_to_all | solution.py:198
  160.7 0.2 select_reduce_fusion.1
  160.9 0.1 compare_convert_fusion
  160.9 9.7 %all-to-all-done.1 = f32[128,1,224]{2,1,0:T(1,128)S(1)} async-done(((f32[128,1,224]{2,1,0:T(1,128)}), f32[128,1,224]{2,1,0:T(1,128)S(1)}, u32[]{:S(2)}, u32[]{:S(2)}) %all-to-all-start.1) | async-done | bytes 114720 | tf_op jit(solution)/shard_map/all_to_all | solution.py:198
  170.7 0.2 reduce_sum.30
  170.8 0.1 subtract_multiply_fusion
  171.0 0.1 reshape.197
  171.1 0.1 copy.40
  171.2 0.6 multiply_bitcast_fusion
  171.8 0.6 copy.41
  (17 shorter events, 0.3 us)
Async XLA Ops:
  2.8 21.2 %all-to-all-start = ((f32[128,1,64]{2,1,0:T(1,128)}), f32[128,1,64]{2,1,0:T(1,128)S(1)}, u32[]{:S(2)}, u32[]{:S(2)}) async-start(f32[128,1,64]{2,1,0:T(1,128)} %broadcast_in_dim.93), calls=%async_computation | async-start | bytes 131072 | tf_op jit(solution)/shard_map/all_to_all | solution.py:170
  156.4 14.3 %all-to-all-start.1 = ((f32[128,1,224]{2,1,0:T(1,128)}), f32[128,1,224]{2,1,0:T(1,128)S(1)}, u32[]{:S(2)}, u32[]{:S(2)}) async-start(f32[128,1,224]{2,1,0:T(1,128)} %shard_map.77), calls=%async_computation.1 | async-start | bytes 262144 | tf_op jit(solution)/shard_map/all_to_all | solution.py:198

commit v13 on v12

--- a/solution.py
+++ b/solution.py
@@ -177,15 +177,19 @@
     coords = grouped[:, :, : 3 * slot_cap].reshape(groups, group_cells, 3, slot_cap)
     per_device = cell_total * slot_cap
     index = jnp.arange(per_device, dtype=jnp.int32)[:, None]
-    peer = jnp.arange(devices, dtype=jnp.int32)[None, :]
-    wanted = (peer % col_devs) * cell_total + index % cell_total
-    within_peer = jnp.repeat(within, col_devs, axis=0)
-    chosen = within_peer[None, :, :] == wanted[:, :, None]
-    coords_peer = jnp.repeat(coords, col_devs, axis=0).transpose(2, 3, 0, 1)
-    picked = coords_peer[:, 0][:, None]
+    member = jnp.arange(col_devs, dtype=jnp.int32)[None, :]
+    wanted = member * cell_total + index % cell_total
+    chosen = within[None, :, None, :] == wanted[:, None, :, None]
+    coords_slot = coords.transpose(2, 3, 0, 1)
+    picked = coords_slot[:, 0][:, None, :, None, :]
     for slot in range(1, slot_cap):
-        picked = jnp.where((index // cell_total == slot)[None, :, :, None], coords_peer[:, slot][:, None], picked)
+        picked = jnp.where(
+            (index // cell_total == slot)[None, :, :, None, None][:, :, :1],
+            coords_slot[:, slot][:, None, :, None, :],
+            picked,
+        )
     target_pos = jnp.sum(jnp.where(chosen[None], picked, 0.0), axis=-1)
+    target_pos = target_pos.reshape(3, per_device, devices)
     device = lax.axis_index("row") * col_devs + lax.axis_index("col")
     own_group = lax.dynamic_index_in_dim(grouped, device // col_devs, 0, keepdims=False)
     own_within = lax.dynamic_index_in_dim(within, device // col_devs, 0, keepdims=False)

time: 173 us -> 173 us (level)
  no operation moved by 1% of the time
where the time goes in v13:
time: 173 us
  Pallas kernels  119 us (69%)
  waiting for transfers between devices  17.3 us (10%)
  starting transfers between devices  15.7 us (9%)
  local copies, waits for them, and re-layouts  14.3 us (8%)
  other arithmetic  6.44 us (4%)
    pallas_call x1, Pallas kernels, pair_sums(): pl.pallas_call(pair_kernel, grid=(source_total // chunk,), in_specs=[pl.B...  119 us
    all_to_all x1, starting transfers between devices, per_device(): every_cell = lax.all_to_all(copies, axes, 0, 0, tiled=True)  11.5 us
    broadcast_in_dim x1, local copies, waits for them, and re-layouts, spread_sources(): return jnp.broadcast_to(sources[:, :, None], sources.shape + (128,))  10 us
    all_to_all x1, waiting for transfers between devices, per_device(): lax.all_to_all(by_device, axes, 0, 0, tiled=True)  9.75 us
    all_to_all x1, waiting for transfers between devices, per_device(): every_cell = lax.all_to_all(copies, axes, 0, 0, tiled=True)  7.59 us
    all_to_all x1, starting transfers between devices, per_device(): lax.all_to_all(by_device, axes, 0, 0, tiled=True)  4.25 us
  transfers between devices with their start and end apart: 2, of which 2 were waited for; matrix products, arithmetic and copies ran while one was open for 1% of the time, Pallas kernels for 0%

profile of v13, /device:TPU:1, one launch (start us, length us, event | category | flops | bytes accessed | tf_op | source)
XLA Modules:
  0.0 173.2 jit_solution(17840440593111108606)
XLA Ops:
  0.6 0.7 reshape.206
  1.3 0.7 convert_bitcast_fusion
  2.0 0.1 copy.28
  2.1 0.1 broadcast_in_dim.95
  2.2 0.7 broadcast_in_dim.96
  2.8 11.5 %all-to-all-start = ((f32[128,1,64]{2,1,0:T(1,128)}), f32[128,1,64]{2,1,0:T(1,128)S(1)}, u32[]{:S(2)}, u32[]{:S(2)}) async-start(f32[128,1,64]{2,1,0:T(1,128)} %broadcast_in_dim.96), calls=%async_computation | async-start | bytes 131072 | tf_op jit(solution)/shard_map/all_to_all | solution.py:170
  14.4 0.9 mul.117
  15.3 0.1 broadcast_add_fusion
  15.3 1.1 pad_maximum_fusion
  16.4 7.6 %all-to-all-done = f32[128,1,64]{2,1,0:T(1,128)S(1)} async-done(((f32[128,1,64]{2,1,0:T(1,128)}), f32[128,1,64]{2,1,0:T(1,128)S(1)}, u32[]{:S(2)}, u32[]{:S(2)}) %all-to-all-start) | async-done | bytes 32800 | tf_op jit(solution)/shard_map/all_to_all | solution.py:170
  24.0 10.0 %broadcast_in_dim.97.source_ref = f32[7,8192,128]{2,1,0:T(8,128)} broadcast(f32[7,8192]{1,0:T(8,128)S(1)} %pad_maximum_fusion), dimensions={0,1} | broadcast | bytes 29589504 | tf_op jit(solution)/shard_map/broadcast_in_dim | solution.py:98
  34.1 0.5 broadcast.259
  34.6 0.8 reduce.6
  35.4 0.2 reshape_reshape.3
  35.6 0.5 fusion
  36.2 0.2 copy.29
  36.5 0.2 broadcast_compare_fusion
  36.7 0.1 broadcast_select_fusion
  36.8 0.9 select_reduce_fusion
  37.7 0.2 copy.30
  37.9 0.7 copy.31.target_ref
  38.6 118.5 %shard_map.77 = f32[128,1,224]{2,1,0:T(1,128)} custom-call(f32[7,8192,128]{2,1,0:T(8,128)} %broadcast_in_dim.97.source_ref, f32[3,16,128]{2,1,0:T(8,128)} %copy.31.target_ref), custom_call_target="tpu_custom_call" | custom-call | tf_op jit(solution)/shard_map/pallas_call | solution.py:105
  157.2 4.2 %all-to-all-start.1 = ((f32[128,1,224]{2,1,0:T(1,128)}), f32[128,1,224]{2,1,0:T(1,128)S(1)}, u32[]{:S(2)}, u32[]{:S(2)}) async-start(f32[128,1,224]{2,1,0:T(1,128)} %shard_map.77), calls=%async_computation.1 | async-start | bytes 262144 | tf_op jit(solution)/shard_map/all_to_all | solution.py:202
  161.4 0.2 select_reduce_fusion.1
  161.6 0.1 compare_convert_fusion
  161.7 9.7 %all-to-all-done.1 = f32[128,1,224]{2,1,0:T(1,128)S(1)} async-done(((f32[128,1,224]{2,1,0:T(1,128)}), f32[128,1,224]{2,1,0:T(1,128)S(1)}, u32[]{:S(2)}, u32[]{:S(2)}) %all-to-all-start.1) | async-done | bytes 114720 | tf_op jit(solution)/shard_map/all_to_all | solution.py:202
  171.4 0.2 reduce_sum.30
  171.6 0.1 subtract_multiply_fusion
  171.7 0.1 reshape.209
  171.8 0.1 copy.33
  171.9 0.6 multiply_bitcast_fusion
  172.5 0.6 copy.34
  (15 shorter events, 0.3 us)
Async XLA Ops:
  2.8 21.2 %all-to-all-start = ((f32[128,1,64]{2,1,0:T(1,128)}), f32[128,1,64]{2,1,0:T(1,128)S(1)}, u32[]{:S(2)}, u32[]{:S(2)}) async-start(f32[128,1,64]{2,1,0:T(1,128)} %broadcast_in_dim.96), calls=%async_computation | async-start | bytes 131072 | tf_op jit(solution)/shard_map/all_to_all | solution.py:170
  157.2 14.3 %all-to-all-start.1 = ((f32[128,1,224]{2,1,0:T(1,128)}), f32[128,1,224]{2,1,0:T(1,128)S(1)}, u32[]{:S(2)}, u32[]{:S(2)}) async-start(f32[128,1,224]{2,1,0:T(1,128)} %shard_map.77), calls=%async_computation.1 | async-start | bytes 262144 | tf_op jit(solution)/shard_map/all_to_all | solution.py:202

commit v14 on v12

--- a/solution.py
+++ b/solution.py
@@ -101,7 +101,7 @@
 def pair_sums(targets, sources):
     per_device, devices = targets.shape[1:]
     source_total = sources.shape[1]
-    chunk = math.gcd(source_total, 1024)
+    chunk = math.gcd(source_total, 512)
     return pl.pallas_call(
         pair_kernel,
         grid=(source_total // chunk,),

time: 173 us -> 172 us (level)
  no operation moved by 1% of the time
where the time goes in v14:
time: 172 us
  Pallas kernels  118 us (69%)
  waiting for transfers between devices  17.3 us (10%)
  starting transfers between devices  15.7 us (9%)
  local copies, waits for them, and re-layouts  13.7 us (8%)
  other arithmetic  6.24 us (4%)
    pallas_call x1, Pallas kernels, pair_sums(): pl.pallas_call(pair_kernel, grid=(source_total // chunk,), in_specs=[pl.B...  118 us
    all_to_all x1, starting transfers between devices, per_device(): every_cell = lax.all_to_all(copies, axes, 0, 0, tiled=True)  11.5 us
    broadcast_in_dim x1, local copies, waits for them, and re-layouts, spread_sources(): return jnp.broadcast_to(sources[:, :, None], sources.shape + (128,))  10 us
    all_to_all x1, waiting for transfers between devices, per_device(): lax.all_to_all(by_device, axes, 0, 0, tiled=True)  9.75 us
    all_to_all x1, waiting for transfers between devices, per_device(): every_cell = lax.all_to_all(copies, axes, 0, 0, tiled=True)  7.59 us
    all_to_all x1, starting transfers between devices, per_device(): lax.all_to_all(by_device, axes, 0, 0, tiled=True)  4.25 us
  transfers between devices with their start and end apart: 2, of which 2 were waited for; matrix products, arithmetic and copies ran while one was open for 1% of the time, Pallas kernels for 0%

profile of v14, /device:TPU:1, one launch (start us, length us, event | category | flops | bytes accessed | tf_op | source)
XLA Modules:
  0.0 172.2 jit_solution(606046576859346275)
XLA Ops:
  0.6 0.7 reshape.194
  1.3 0.7 convert_bitcast_fusion
  2.0 0.1 copy.34
  2.1 0.1 broadcast_in_dim.92
  2.2 0.7 broadcast_in_dim.93
  2.8 11.5 %all-to-all-start = ((f32[128,1,64]{2,1,0:T(1,128)}), f32[128,1,64]{2,1,0:T(1,128)S(1)}, u32[]{:S(2)}, u32[]{:S(2)}) async-start(f32[128,1,64]{2,1,0:T(1,128)} %broadcast_in_dim.93), calls=%async_computation | async-start | bytes 131072 | tf_op jit(solution)/shard_map/all_to_all | solution.py:170
  14.4 0.9 mul.118
  15.3 0.1 broadcast_add_fusion
  15.3 1.1 pad_maximum_fusion
  16.4 7.6 %all-to-all-done = f32[128,1,64]{2,1,0:T(1,128)S(1)} async-done(((f32[128,1,64]{2,1,0:T(1,128)}), f32[128,1,64]{2,1,0:T(1,128)S(1)}, u32[]{:S(2)}, u32[]{:S(2)}) %all-to-all-start) | async-done | bytes 32800 | tf_op jit(solution)/shard_map/all_to_all | solution.py:170
  24.0 10.0 %broadcast_in_dim.94.source_ref = f32[7,8192,128]{2,1,0:T(8,128)} broadcast(f32[7,8192]{1,0:T(8,128)S(1)} %pad_maximum_fusion), dimensions={0,1} | broadcast | bytes 29589504 | tf_op jit(solution)/shard_map/broadcast_in_dim | solution.py:98
  34.1 0.5 broadcast.238
  34.6 0.8 reduce.6
  35.4 0.2 reshape_reshape.3
  35.6 0.5 fusion
  36.2 0.2 copy.36
  36.5 0.1 copy.35
  36.6 0.1 copy.37
  36.7 0.1 copy.38
  36.9 0.1 broadcast_compare_fusion
  36.9 1.0 select_reduce_fusion.target_ref
  37.9 118.3 %shard_map.77 = f32[128,1,224]{2,1,0:T(1,128)} custom-call(f32[7,8192,128]{2,1,0:T(8,128)} %broadcast_in_dim.94.source_ref, f32[3,16,128]{2,1,0:T(8,128)} %select_reduce_fusion.target_ref), custom_call_target="tpu_custom_call" | custom-call | tf_op jit(solution)/shard_map/pallas_call | solution.py:105
  156.2 4.2 %all-to-all-start.1 = ((f32[128,1,224]{2,1,0:T(1,128)}), f32[128,1,224]{2,1,0:T(1,128)S(1)}, u32[]{:S(2)}, u32[]{:S(2)}) async-start(f32[128,1,224]{2,1,0:T(1,128)} %shard_map.77), calls=%async_computation.1 | async-start | bytes 262144 | tf_op jit(solution)/shard_map/all_to_all | solution.py:198
  160.4 0.2 select_reduce_fusion.1
  160.6 0.1 compare_convert_fusion
  160.7 9.7 %all-to-all-done.1 = f32[128,1,224]{2,1,0:T(1,128)S(1)} async-done(((f32[128,1,224]{2,1,0:T(1,128)}), f32[128,1,224]{2,1,0:T(1,128)S(1)}, u32[]{:S(2)}, u32[]{:S(2)}) %all-to-all-start.1) | async-done | bytes 114720 | tf_op jit(solution)/shard_map/all_to_all | solution.py:198
  170.4 0.2 reduce_sum.30
  170.6 0.1 subtract_multiply_fusion
  170.7 0.1 reshape.197
  170.8 0.1 copy.40
  170.9 0.6 multiply_bitcast_fusion
  171.6 0.6 copy.41
  (17 shorter events, 0.3 us)
Async XLA Ops:
  2.8 21.2 %all-to-all-start = ((f32[128,1,64]{2,1,0:T(1,128)}), f32[128,1,64]{2,1,0:T(1,128)S(1)}, u32[]{:S(2)}, u32[]{:S(2)}) async-start(f32[128,1,64]{2,1,0:T(1,128)} %broadcast_in_dim.93), calls=%async_computation | async-start | bytes 131072 | tf_op jit(solution)/shard_map/all_to_all | solution.py:170
  156.2 14.3 %all-to-all-start.1 = ((f32[128,1,224]{2,1,0:T(1,128)}), f32[128,1,224]{2,1,0:T(1,128)S(1)}, u32[]{:S(2)}, u32[]{:S(2)}) async-start(f32[128,1,224]{2,1,0:T(1,128)} %shard_map.77), calls=%async_computation.1 | async-start | bytes 262144 | tf_op jit(solution)/shard_map/all_to_all | solution.py:198
